TPU v7x, 512 devices: a whole 4x4x16 slice. The times are simulated.
512 devices in a mesh: clip: 4 (over y), st: 32 (over x_hi, z), fsdp: 4 (over x_lo, core).
Axes of the slice: x: 4 (x_hi: 2, x_lo: 2; x = x_hi * 2 + x_lo), y: 4, z: 16, core: 2. Of those that a mesh axis runs over, the one named last changes fastest.
Arguments:
- clip_tokens: bfloat16 [1024, 128, 1024], P(('clip', 'st'), 'fsdp'), parts along dimension 0, may hold values from -6 to 6
- w_spatial: bfloat16 [9, 1024, 512], P(None, ('st', 'fsdp')), may hold values from -0.0625 to 0.0625
- w_temporal: bfloat16 [3, 512, 1024], P(None, None, ('st', 'fsdp')), may hold values from -0.15625 to 0.15625
- frame_time: int32 [64], P('clip'), parts along dimension 0, may hold values from 0 to 15, each once
- dilation: int32 [32], P('clip'), parts along dimension 0, may hold values from 1 to 3
Outputs:
- block_out: bfloat16 [1024, 128, 1024], P(('clip', 'st'), 'fsdp'), parts along dimension 0
There are 4 independent parts, one for each index of `clip`. A program takes and returns all parts, laid end to end along the dimension named above; an argument that names none is the same for every part. Nothing has to cross between parts.
Inputs may be any that keep to these rules, and one draw needn't show every extreme that they name: frame_time is a permutation of 0 to 15.
All inputs are finite; a program needn't handle non-finite values.
Results may differ from a plain program's by a relative error of at most 0.0049.
Values may be sent and summed in bfloat16 or wider, within the bound.
No kernel may reach another device: no remote copies, remote signals or barrier semaphores. Data moves between devices by JAX's collectives and lax.ppermute only.
A program may use at most 64 MiB of HBM per device.

v0:
```python
import jax
import jax.numpy as jnp
from jax import lax
from jax.sharding import PartitionSpec as P

DGROUPS = 8
FRAMES = 16
ROWS = 16


def padded_2(cells, sides, width):
    for axis, dim in sides:
        count = lax.axis_size(axis)
        ends = count - 1
        head = lax.slice_in_dim(cells, 0, width, axis=dim)
        tail = lax.slice_in_dim(cells, cells.shape[dim] - width, cells.shape[dim], axis=dim)
        cells = jnp.concatenate(
            [
                lax.ppermute(tail, axis, [(i, (i + 1) % count) for i in range(ends)]),
                cells,
                lax.ppermute(head, axis, [((i + 1) % count, i) for i in range(ends)]),
            ],
            axis=dim,
        )
    return cells


def partner(value, axis, distance):
    mask = 2**distance
    pairs = [(source, source ^ mask) for source in range(lax.axis_size(axis))]
    return lax.ppermute(value, axis, pairs)


def shards(clip_tokens, w_spatial, w_temporal, frame_time, dilation):
    rows_dev, cols_dev, channels = clip_tokens.shape
    middle = w_spatial.shape[2]
    group_size = lax.axis_size("st")
    values = clip_tokens.astype(jnp.float32)
    average = jnp.mean(values, axis=-1, keepdims=True)
    kernel_extent = jnp.mean(jnp.square(values - average), axis=-1, keepdims=True)
    normed = ((values - average) * lax.rsqrt(kernel_extent + 1e-06)).astype(jnp.bfloat16)
    widened = padded_2(normed, (("fsdp", 1),), 1)
    blank_row = jnp.zeros((1,) + widened.shape[1:], jnp.bfloat16)
    lower_half = lax.axis_index("st") % 2 == 1
    outgoing = jnp.where(lower_half, widened[:1], widened[-1:])
    incoming = partner(outgoing, "st", 0)
    top_rim = jnp.where(lower_half, incoming, blank_row)
    bottom_rim = jnp.where(lower_half, blank_row, incoming)
    padded = jnp.concatenate([top_rim, widened, bottom_rim], axis=0)
    first_row = lax.axis_index("st") * rows_dev
    in_frame = (first_row + jnp.arange(rows_dev, dtype=jnp.int32)) % ROWS
    windows = []
    for shift_amount in (-1, 0, 1):
        inside = ((in_frame + shift_amount >= 0) & (in_frame + shift_amount < ROWS)).astype(
            jnp.bfloat16
        )
        windows.append(
            padded[1 + shift_amount : 1 + shift_amount + rows_dev] * inside[:, None, None]
        )
    tokens = rows_dev * cols_dev
    initial = jnp.zeros((tokens, middle), jnp.float32)
    running = initial
    portion = lax.all_gather(w_spatial, ("st", "fsdp"), axis=1, tiled=True)
    span = portion.shape[1]
    for row_tap in range(3):
        for column_kernel_tap in range(3):
            patches = windows[row_tap][:, column_kernel_tap : column_kernel_tap + cols_dev, :]
            running = running + jnp.dot(
                patches.reshape(tokens, span),
                portion[3 * row_tap + column_kernel_tap],
                preferred_element_type=jnp.float32,
            )
    hidden = jax.nn.gelu(running).astype(jnp.bfloat16)
    pixel_values = ROWS * cols_dev
    block_length_span = min(tokens, pixel_values) // group_size
    depth_len = tokens // (group_size * block_length_span)
    arrived = lax.all_to_all(
        hidden.reshape(depth_len, group_size, block_length_span, middle),
        "st",
        split_axis=1,
        concat_axis=0,
        tiled=True,
    )
    per_pixel = pixel_values // group_size
    group_width = middle // DGROUPS
    frame_sequence = arrived.reshape(FRAMES, per_pixel, DGROUPS, group_width)
    offsets = (jnp.arange(3, dtype=jnp.int32) - 1)[None, :] * dilation[:, None]
    selector_matrix = (
        frame_time[None, None, None, :]
        == frame_time[None, None, :, None] + offsets[:, :, None, None]
    ).astype(jnp.bfloat16)
    stacked_panels = jnp.einsum(
        "gkfe,epgc->kfpgc", selector_matrix, frame_sequence, preferred_element_type=jnp.float32
    )
    stacked_panels = stacked_panels.astype(jnp.bfloat16).reshape(3, FRAMES * per_pixel, middle)
    portion = lax.all_gather(w_temporal, ("st", "fsdp"), axis=2, tiled=True)
    result = jnp.dot(stacked_panels[0], portion[0], preferred_element_type=jnp.float32)
    result = result + jnp.dot(stacked_panels[1], portion[1], preferred_element_type=jnp.float32)
    mixed_out = (
        result + jnp.dot(stacked_panels[2], portion[2], preferred_element_type=jnp.float32)
    ).astype(jnp.bfloat16)
    returned = lax.all_to_all(
        mixed_out.reshape(group_size, depth_len, 1, block_length_span, channels),
        "st",
        split_axis=0,
        concat_axis=2,
        tiled=True,
    )
    update = returned.reshape(rows_dev, cols_dev, channels)
    return (values + update.astype(jnp.float32)).astype(jnp.bfloat16)


def solution(mesh):
    return jax.shard_map(
        shards,
        mesh=mesh,
        in_specs=(
            P(("clip", "st"), "fsdp", None),
            P(None, ("st", "fsdp"), None),
            P(None, None, ("st", "fsdp")),
            P("clip"),
            P("clip"),
        ),
        out_specs=P(("clip", "st"), "fsdp", None),
        check_vma=False,
    )
```

profile of v0, /device:TPU:1, one launch (start us, length us, event | category | flops | bytes accessed | tf_op | source)
XLA Modules:
  0.0 521.0 jit_solution(9462733615842802531)
XLA Ops:
  6.5 0.7 all-gather.3.cloned.1.call-update
  7.3 0.7 all-gather.5.cloned.1.call-update
  8.0 1.2 convert_reduce_fusion
  9.2 1.3 fusion.5
  10.5 1.3 fusion.6
  11.9 4.5 collective-permute-start
  16.4 5.6 %collective-permute-start.1 = (bf16[8,1,1024]{2,1,0:T(2,128)(2,1)S(1)}, bf16[8,1,1024]{2,1,0:T(2,128)(2,1)S(1)}, u32[]{:S(2)}, u32[]{:S(2)}) collective-permute-start(bf16[8,1,1024]{2,1,0:T(2,128)(2,1)S(1)} %get-tuple-element.21), channel_id=1, source_target_pairs={{1,0},{2,1},{3,2},{5,4},{6,5},{7,6},{9,8},{10,9},{11,10},{13,12},{... | collective-permute-start | bytes 49160 | tf_op jit(solution)/shard_map/ppermute | solution.py:21
  22.0 0.8 collective-permute-done.1
  23.1 2.4 collective-permute-start.2
  25.5 3.2 collective-permute-done.2
  28.7 0.7 fusion.10
  29.4 1.2 fusion.30
  30.9 1.1 fusion.28
  32.0 212.3 %all-gather.3.cloned.1.call-done = bf16[9,1024,512]{2,1,0:T(8,128)(2,1)} async-done(((bf16[9,8,512]{2,1,0:T(8,128)(2,1)}), bf16[9,1024,512]{2,1,0:T(8,128)(2,1)}) %all-gather.3.cloned.1.call-update) | async-done | bytes 9437200 | tf_op jit(solution)/shard_map/all_gather | solution.py:63
  244.4 2.0 fusion.9
  246.3 2.4 convolution_add_fusion.9
  248.7 1.7 convolution_add_fusion.8
  250.4 1.7 convolution_add_fusion.7
  252.1 0.4 convolution_add_fusion.6
  253.0 0.4 convolution_add_fusion.4
  253.4 0.4 convolution_add_fusion.3
  253.9 0.6 copy-done.3
  254.5 1.3 fusion.20
  255.7 10.0 %all-to-all-start = ((bf16[1,32,8,512]{3,2,0,1:T(8,128)(2,1)}), bf16[1,32,8,512]{3,2,0,1:T(8,128)(2,1)S(1)}, u32[]{:S(2)}, u32[]{:S(2)}) async-start(bf16[1,32,8,512]{3,2,0,1:T(8,128)(2,1)} %fusion.20), calls=%async_computation | async-start | bytes 524288 | tf_op jit(solution)/shard_map/all_to_all | solution.py:77
  265.9 20.3 %all-to-all-done = bf16[1,32,8,512]{3,2,0,1:T(8,128)(2,1)S(1)} async-done(((bf16[1,32,8,512]{3,2,0,1:T(8,128)(2,1)}), bf16[1,32,8,512]{3,2,0,1:T(8,128)(2,1)S(1)}, u32[]{:S(2)}, u32[]{:S(2)}) %all-to-all-start) | async-done | bytes 262176 | tf_op jit(solution)/shard_map/all_to_all | solution.py:77
  286.5 0.9 fusion
  289.7 178.6 %all-gather.5.cloned.1.call-done = bf16[3,512,1024]{1,2,0:T(8,128)(2,1)} async-done(((bf16[3,512,8]{1,2,0:T(8,128)(2,1)}), bf16[3,512,1024]{1,2,0:T(8,128)(2,1)}) %all-gather.5.cloned.1.call-update) | async-done | bytes 3145744 | tf_op jit(solution)/shard_map/all_gather | solution.py:96
  468.3 1.7 fusion.8
  470.0 1.7 convolution_add_fusion.1
  471.7 1.8 fusion.4
  473.5 39.7 %all_to_all.8 = bf16[32,1,1,8,1024]{4,3,2,1,0:T(8,128)(2,1)S(1)} all-to-all(bf16[32,1,1,8,1024]{4,3,2,1,0:T(8,128)(2,1)S(1)} %fusion.4), channel_id=1, replica_groups=mesh['clip'=4,'st'=32,'fsdp'=4] {'st'}, dimensions={0} | all-to-all | bytes 1048576 | tf_op jit(solution)/shard_map/all_to_all | solution.py:102
  513.2 1.0 fusion.7
  (35 shorter events, 3.8 us)
Async XLA Ops:
  6.5 237.8 %all-gather.3.cloned.1.call-start = ((), (), s32[]{:S(2)}) async-start(), calls=%async_computation.2 | async-start | bytes 9510912 | tf_op jit(solution)/shard_map/all_gather | solution.py:63
  7.3 461.1 %all-gather.5.cloned.1.call-start = ((), (), s32[]{:S(2)}) async-start(), calls=%async_computation.3 | async-start | bytes 3170304 | tf_op jit(solution)/shard_map/all_gather | solution.py:96
  11.9 10.1 %collective-permute-start = (bf16[8,1,1024]{2,1,0:T(2,128)(2,1)S(1)}, bf16[8,1,1024]{2,1,0:T(2,128)(2,1)S(1)}, u32[]{:S(2)}, u32[]{:S(2)}) collective-permute-start(bf16[8,1,1024]{2,1,0:T(2,128)(2,1)S(1)} %get-tuple-element.20), channel_id=1, source_target_pairs={{0,1},{1,2},{2,3},{4,5},{5,6},{6,7},{8,9},{9,10},{10,11},{12,13},{... | collective-permute-start | bytes 49160 | tf_op jit(solution)/shard_map/ppermute | solution.py:19
  16.4 6.4 %collective-permute-start.1 = (bf16[8,1,1024]{2,1,0:T(2,128)(2,1)S(1)}, bf16[8,1,1024]{2,1,0:T(2,128)(2,1)S(1)}, u32[]{:S(2)}, u32[]{:S(2)}) collective-permute-start(bf16[8,1,1024]{2,1,0:T(2,128)(2,1)S(1)} %get-tuple-element.21), channel_id=1, source_target_pairs={{1,0},{2,1},{3,2},{5,4},{6,5},{7,6},{9,8},{10,9},{11,10},{13,12},{... | collective-permute-start | bytes 49160 | tf_op jit(solution)/shard_map/ppermute | solution.py:21
  23.1 5.6 %collective-permute-start.2 = (bf16[1,34,1024]{2,1,0:T(8,128)(2,1)S(1)}, bf16[1,34,1024]{2,1,0:T(8,128)(2,1)S(1)}, u32[]{:S(2)}, u32[]{:S(2)}) collective-permute-start(bf16[1,34,1024]{2,1,0:T(8,128)(2,1)S(1)} %slice_select_fusion), channel_id=1, source_target_pairs={{0,4},{4,0},{8,12},{12,8},{16,20},{20,16},{24,28},{28,24},{32,36},... | collective-permute-start | bytes 208904 | tf_op jit(solution)/shard_map/ppermute | solution.py:31
  244.3 2.0 copy-start.2
  244.3 7.7 %copy-start.1 = (bf16[9,1024,512]{2,1,0:T(8,128)(2,1)S(1)}, bf16[9,1024,512]{2,1,0:T(8,128)(2,1)}, u32[]{:S(2)}) copy-start(bf16[9,1024,512]{2,1,0:T(8,128)(2,1)} %all-gather.3.cloned.1.call-done) | copy-start | bytes 28311556
  253.4 1.0 copy-start.3
  254.5 11.3 %copy-start.5 = (s32[8]{0:T(128)S(1)}, s32[8]{0:T(128)}, u32[]{:S(2)}) copy-start(s32[8]{0:T(128)} %param.9) | copy-start | bytes 100
  254.5 11.4 %copy-start.4 = (s32[16]{0:T(128)S(1)}, s32[16]{0:T(128)}, u32[]{:S(2)}) copy-start(s32[16]{0:T(128)} %param.8) | copy-start | bytes 196
  255.7 30.5 %all-to-all-start = ((bf16[1,32,8,512]{3,2,0,1:T(8,128)(2,1)}), bf16[1,32,8,512]{3,2,0,1:T(8,128)(2,1)S(1)}, u32[]{:S(2)}, u32[]{:S(2)}) async-start(bf16[1,32,8,512]{3,2,0,1:T(8,128)(2,1)} %fusion.20), calls=%async_computation | async-start | bytes 524288 | tf_op jit(solution)/shard_map/all_to_all | solution.py:77
  471.7 41.5 %copy-start = (bf16[8,32,1024]{2,1,0:T(8,128)(2,1)S(1)}, bf16[8,32,1024]{2,1,0:T(8,128)(2,1)}, u32[]{:S(2)}) copy-start(bf16[8,32,1024]{2,1,0:T(8,128)(2,1)} %param.5) | copy-start | bytes 1572868
Sparse Core Ops, SparseCore 0:
  9.5 234.7 all-gather.2
  246.5 221.7 all-gather.4
where the time goes:
time: 524 us; the launch traced here: 521 us
  waiting for transfers between devices  417 us (80%)
  blocking collectives  39.7 us (8%)
  starting transfers between devices  22.5 us (4%)
  matrix products  16.7 us (3%)
  between operations  13.7 us (3%)
  other arithmetic  5.9 us (1%)
  local copies, waits for them, and re-layouts  5.82 us (1%)
    all_gather x1, waiting for transfers between devices, shards(): portion = lax.all_gather(w_spatial, ('st', 'fsdp'), axis=1, tiled=True)  212 us
    all_gather x1, waiting for transfers between devices, shards(): portion = lax.all_gather(w_temporal, ('st', 'fsdp'), axis=2, tiled=True)  179 us
    all_to_all x1, blocking collectives, shards(): lax.all_to_all(mixed_out.reshape(group_size, depth_len, 1, block_length_s...  39.7 us
    all_to_all x1, waiting for transfers between devices, shards(): lax.all_to_all(hidden.reshape(depth_len, group_size, block_length_span, m...  20.3 us
    dot_general x9, matrix products, shards(): jnp.dot(patches.reshape(tokens, span), portion[3 * row_tap + column_kerne...  10.7 us
  transfers between devices with their start and end apart: 6, of which 5 were waited for; matrix products, arithmetic and copies ran while one was open for 4% of the time, Pallas kernels for 0%

commit v1 on v0

--- a/solution.py
+++ b/solution.py
@@ -6,6 +6,8 @@
 DGROUPS = 8
 FRAMES = 16
 ROWS = 16
+ST = ("xhi", "z")
+FS = ("xlo", "core")
 
 
 def padded_2(cells, sides, width):
@@ -31,23 +33,47 @@
     return lax.ppermute(value, axis, pairs)
 
 
+def out_dot(panel, weight):
+    return lax.dot_general(
+        panel, weight, (((1,), (1,)), ((), ())), preferred_element_type=jnp.float32
+    )
+
+
+def gathered_weights(w_spatial, w_temporal):
+    taps, block, middle = w_spatial.shape
+    k_taps, _, out_block = w_temporal.shape
+    cut = w_spatial.size
+    flat = jnp.concatenate([w_spatial.reshape(-1), w_temporal.transpose(2, 0, 1).reshape(-1)])
+    whole = lax.all_gather(flat, "z", axis=0)
+    whole = lax.all_gather(whole, ("xhi", "xlo"), axis=0)
+    whole = lax.all_gather(whole, "core", axis=0)
+    n_core, n_x, n_z = whole.shape[:3]
+    n_hi = lax.axis_size("xhi")
+    lead = (n_core, n_hi, n_x // n_hi, n_z)
+    spatial = whole[..., :cut].reshape(lead + (taps, block, middle))
+    spatial = spatial.transpose(4, 1, 3, 2, 0, 5, 6).reshape(taps, -1, middle)
+    temporal = whole[..., cut:].reshape(lead + (out_block, k_taps, middle))
+    temporal = temporal.transpose(5, 1, 3, 2, 0, 4, 6).reshape(k_taps, -1, middle)
+    return spatial, temporal
+
+
 def shards(clip_tokens, w_spatial, w_temporal, frame_time, dilation):
     rows_dev, cols_dev, channels = clip_tokens.shape
     middle = w_spatial.shape[2]
-    group_size = lax.axis_size("st")
+    group_size = lax.axis_size(ST)
     values = clip_tokens.astype(jnp.float32)
     average = jnp.mean(values, axis=-1, keepdims=True)
     kernel_extent = jnp.mean(jnp.square(values - average), axis=-1, keepdims=True)
     normed = ((values - average) * lax.rsqrt(kernel_extent + 1e-06)).astype(jnp.bfloat16)
-    widened = padded_2(normed, (("fsdp", 1),), 1)
+    widened = padded_2(normed, ((FS, 1),), 1)
     blank_row = jnp.zeros((1,) + widened.shape[1:], jnp.bfloat16)
-    lower_half = lax.axis_index("st") % 2 == 1
+    lower_half = lax.axis_index(ST) % 2 == 1
     outgoing = jnp.where(lower_half, widened[:1], widened[-1:])
-    incoming = partner(outgoing, "st", 0)
+    incoming = partner(outgoing, ST, 0)
     top_rim = jnp.where(lower_half, incoming, blank_row)
     bottom_rim = jnp.where(lower_half, blank_row, incoming)
     padded = jnp.concatenate([top_rim, widened, bottom_rim], axis=0)
-    first_row = lax.axis_index("st") * rows_dev
+    first_row = lax.axis_index(ST) * rows_dev
     in_frame = (first_row + jnp.arange(rows_dev, dtype=jnp.int32)) % ROWS
     windows = []
     for shift_amount in (-1, 0, 1):
@@ -60,7 +86,8 @@
     tokens = rows_dev * cols_dev
     initial = jnp.zeros((tokens, middle), jnp.float32)
     running = initial
-    portion = lax.all_gather(w_spatial, ("st", "fsdp"), axis=1, tiled=True)
+    spatial_w, temporal_w = gathered_weights(w_spatial, w_temporal)
+    portion = spatial_w
     span = portion.shape[1]
     for row_tap in range(3):
         for column_kernel_tap in range(3):
@@ -76,7 +103,7 @@
     depth_len = tokens // (group_size * block_length_span)
     arrived = lax.all_to_all(
         hidden.reshape(depth_len, group_size, block_length_span, middle),
-        "st",
+        ST,
         split_axis=1,
         concat_axis=0,
         tiled=True,
@@ -93,15 +120,13 @@
         "gkfe,epgc->kfpgc", selector_matrix, frame_sequence, preferred_element_type=jnp.float32
     )
     stacked_panels = stacked_panels.astype(jnp.bfloat16).reshape(3, FRAMES * per_pixel, middle)
-    portion = lax.all_gather(w_temporal, ("st", "fsdp"), axis=2, tiled=True)
-    result = jnp.dot(stacked_panels[0], portion[0], preferred_element_type=jnp.float32)
-    result = result + jnp.dot(stacked_panels[1], portion[1], preferred_element_type=jnp.float32)
-    mixed_out = (
-        result + jnp.dot(stacked_panels[2], portion[2], preferred_element_type=jnp.float32)
-    ).astype(jnp.bfloat16)
+    portion = temporal_w
+    result = out_dot(stacked_panels[0], portion[0])
+    result = result + out_dot(stacked_panels[1], portion[1])
+    mixed_out = (result + out_dot(stacked_panels[2], portion[2])).astype(jnp.bfloat16)
     returned = lax.all_to_all(
         mixed_out.reshape(group_size, depth_len, 1, block_length_span, channels),
-        "st",
+        ST,
         split_axis=0,
         concat_axis=2,
         tiled=True,
@@ -111,16 +136,20 @@
 
 
 def solution(mesh):
+    clips = mesh.shape["clip"]
+    fine = jax.sharding.Mesh(
+        mesh.devices.reshape(clips, 2, -1, 2, 2), ("clip", "xhi", "z", "xlo", "core")
+    )
     return jax.shard_map(
         shards,
-        mesh=mesh,
+        mesh=fine,
         in_specs=(
-            P(("clip", "st"), "fsdp", None),
-            P(None, ("st", "fsdp"), None),
-            P(None, None, ("st", "fsdp")),
+            P(("clip", "xhi", "z"), ("xlo", "core"), None),
+            P(None, ("xhi", "z", "xlo", "core"), None),
+            P(None, None, ("xhi", "z", "xlo", "core")),
             P("clip"),
             P("clip"),
         ),
-        out_specs=P(("clip", "st"), "fsdp", None),
+        out_specs=P(("clip", "xhi", "z"), ("xlo", "core"), None),
         check_vma=False,
     )

time: 524 us -> 342 us (0.65)
  waiting for transfers between devices: 417 us -> 176 us
  local copies, waits for them, and re-layouts: 5.82 us -> 73.8 us
  matrix products: 16.7 us -> 8.11 us
    all_gather x2 -> x3, waiting for transfers between devices: 391 us -> 168 us  [the longest x1 80.1 us: gathered_weights(): whole = lax.all_gather(whole, ('xhi', 'xlo'), axis=0)]
    slice x2 -> x18, local copies, waits for them, and re-layouts: 0.69 us -> 32.1 us  [the longest x2 11.7 us: shards(): portion[2]]
    unnamed x12 -> x32, local copies, waits for them, and re-layouts: 0.61 us -> 19.2 us
    all_to_all x1, waiting for transfers between devices: 20.3 us -> 3.57 us  [shards(): lax.all_to_all(hidden.reshape(depth_len, group_size, block_length_span, m...]
    reshape x0 -> x2, local copies, waits for them, and re-layouts: none -> 6.04 us  [the longest x1 6.01 us: gathered_weights(): temporal = whole[..., cut:].reshape(lead + (out_block, k_taps, middle))]
    dot_general x9, matrix products: 10.7 us -> 4.81 us  [shards(): jnp.dot(patches.reshape(tokens, span), portion[3 * row_tap + column_kerne...]
  transfers between devices with their start and end apart: 6 -> 7, of which waited for: 5 -> 6; matrix products, arithmetic and copies ran while one was open for 4% -> 7% of each run, Pallas kernels for 0% -> 0%
where the time goes in v1:
time: 342 us; the launch traced here: 340 us
  waiting for transfers between devices  176 us (51%)
  local copies, waits for them, and re-layouts  73.8 us (22%)
  blocking collectives  42.3 us (12%)
  starting transfers between devices  22.5 us (7%)
  between operations  13.5 us (4%)
  matrix products  8.11 us (2%)
  other arithmetic  3.46 us (1%)
    all_gather x1, waiting for transfers between devices, gathered_weights(): whole = lax.all_gather(whole, ('xhi', 'xlo'), axis=0)  80.1 us
    all_gather x1, waiting for transfers between devices, gathered_weights(): whole = lax.all_gather(flat, 'z', axis=0)  68.4 us
    all_to_all x1, blocking collectives, shards(): lax.all_to_all(mixed_out.reshape(group_size, depth_len, 1, block_length_s...  42.3 us
    unnamed x32, local copies, waits for them, and re-layouts  19.2 us
    all_gather x1, waiting for transfers between devices, gathered_weights(): whole = lax.all_gather(whole, 'core', axis=0)  19.1 us
    all_to_all x1, starting transfers between devices, shards(): lax.all_to_all(hidden.reshape(depth_len, group_size, block_length_span, m...  13.9 us
    slice x2, local copies, waits for them, and re-layouts, shards(): portion[2]  11.7 us
    slice x1, local copies, waits for them, and re-layouts, gathered_weights(): spatial = whole[..., :cut].reshape(lead + (taps, block, middle))  8.1 us
  transfers between devices with their start and end apart: 7, of which 6 were waited for; matrix products, arithmetic and copies ran while one was open for 7% of the time, Pallas kernels for 0%

profile of v1, /device:TPU:1, one launch (start us, length us, event | category | flops | bytes accessed | tf_op | source)
XLA Modules:
  0.0 340.0 jit_solution(10516458373411817871)
XLA Ops:
  9.0 68.4 %all-gather.7.cloned.1.call-done = bf16[786432]{0:T(1024)(128)(2,1)} async-done(((bf16[49152]{0:T(1024)(128)(2,1)}), bf16[786432]{0:T(1024)(128)(2,1)}) %all-gather.7.cloned.1.call-update) | async-done | bytes 1572880 | tf_op jit(solution)/shard_map/all_gather | solution.py:47
  77.4 2.7 reshape.194
  80.2 80.1 %all-gather.9.cloned.1.call-done = bf16[64,49152]{1,0:T(8,128)(2,1)} async-done(((bf16[16,49152]{1,0:T(8,128)(2,1)}), bf16[64,49152]{1,0:T(8,128)(2,1)}) %all-gather.9.cloned.1.call-update) | async-done | bytes 6291472 | tf_op jit(solution)/shard_map/all_gather | solution.py:48
  160.3 1.0 copy-done
  162.1 3.4 collective-permute-start
  165.5 1.9 collective-permute-start.1
  167.6 3.1 collective-permute-done.1
  171.0 3.2 collective-permute-start.2
  174.2 2.0 collective-permute-done.2
  176.9 1.3 fusion.28
  178.2 1.4 fusion.29
  179.6 1.3 fusion.30
  180.9 19.1 %all-gather.11.cloned.1.call-done = bf16[8,16,49152]{2,1,0:T(8,128)(2,1)} async-done(((bf16[4,16,49152]{2,1,0:T(8,128)(2,1)}), bf16[8,16,49152]{2,1,0:T(8,128)(2,1)}) %all-gather.11.cloned.1.call-update) | async-done | bytes 12582928 | tf_op jit(solution)/shard_map/all_gather | solution.py:49
  200.0 2.1 slice.169
  202.1 8.1 %slice.150 = bf16[2,4,16,36864]{3,2,1,0:T(8,128)(2,1)} slice(bf16[2,4,16,49152]{3,2,1,0:T(8,128)(2,1)} %bitcast.92), slice={[0:2], [0:4], [0:16], [0:36864]} | slice | bytes 18874368 | tf_op jit(solution)/shard_map/slice | solution.py:53
  210.2 11.3 %copy.55 = bf16[16,8,72,512]{3,2,1,0:T(8,128)(2,1)} copy(bf16[16,8,72,512]{3,1,2,0:T(8,128)(2,1)} %bitcast.89) | data formatting | bytes 18874368
  221.5 4.1 %fusion.25 = (bf16[1,2,16,2,2,8,512]{6,5,0,2,3,1,4:T(8,128)(2,1)S(1)}, bf16[1,2,16,2,2,8,512]{6,5,0,2,3,1,4:T(8,128)(2,1)S(1)}, bf16[1,2,16,2,2,8,512]{6,5,0,2,3...) fusion(bf16[9,2,16,2,2,8,512]{6,5,0,2,3,1,4:T(8,128)(2,1)} %bit, ...), kind=kLoop, calls=%fused_computation.63 | loop fusion | bytes 18874368 | tf_op jit(solution)/shard_map/slice | solution.py:97
  235.5 1.3 fusion.18
  236.7 13.9 %all-to-all-start = ((bf16[1,32,8,512]{3,2,0,1:T(8,128)(2,1)}), bf16[1,32,8,512]{3,2,0,1:T(8,128)(2,1)S(1)}, u32[]{:S(2)}, u32[]{:S(2)}) async-start(bf16[1,32,8,512]{3,2,0,1:T(8,128)(2,1)} %fusion.18), calls=%async_computation | async-start | bytes 524288 | tf_op jit(solution)/shard_map/all_to_all | solution.py:104
  250.6 6.0 %reshape.191 = bf16[2,2,2,16,8,3,512]{6,5,4,3,2,1,0:T(4,128)(2,1)} reshape(bf16[2,4,16,12288]{3,2,1,0:T(8,128)(2,1)S(1)} %slice.169) | data formatting | bytes 6291456 | tf_op jit(solution)/shard_map/reshape | solution.py:55
  256.6 11.4 %fusion.26 = (bf16[1,2,16,2,2,8,512]{6,0,5,2,3,1,4:T(2,128)(2,1)S(1)}, bf16[1,2,16,2,2,8,512]{6,0,5,2,3,1,4:T(2,128)(2,1)S(1)}, bf16[1,2,16,2,2,8,512]{6,0,5,2,3,1,4:T(2,128)(2,1)S(1)}) fusion(bf16[3,2,16,2,2,8,512]{6,0,5,2,3,1,4:T(4,128)(2,1)} %bitcast.90), kind=kLoop, calls=%fused_computation.64 | loop fusion | bytes 6291456 | tf_op jit(solution)/shard_map/slice | solution.py:126
  269.0 3.6 %all-to-all-done = bf16[1,32,8,512]{3,2,0,1:T(8,128)(2,1)S(1)} async-done(((bf16[1,32,8,512]{3,2,0,1:T(8,128)(2,1)}), bf16[1,32,8,512]{3,2,0,1:T(8,128)(2,1)S(1)}, u32[]{:S(2)}, u32[]{:S(2)}) %all-to-all-start) | async-done | bytes 262176 | tf_op jit(solution)/shard_map/all_to_all | solution.py:104
  272.6 1.1 reshape.190
  273.6 1.9 fusion
  275.5 1.2 fusion.27
  276.8 1.1 copy.47
  277.9 2.1 squeeze.58
  280.0 2.2 copy.45
  282.2 2.1 squeeze.56
  284.3 2.2 copy.43
  286.4 1.4 squeeze.54
  290.2 42.3 %all_to_all.8 = bf16[32,1,1,8,1024]{4,3,2,1,0:T(8,128)(2,1)S(1)} all-to-all(bf16[32,1,1,8,1024]{4,3,2,1,0:T(8,128)(2,1)S(1)} %fusion.4), channel_id=1, replica_groups=mesh['clip'=4,'xhi'=2,'z'=16,'xlo'=2,'core'=2] {'xhi','z'}, dimensions={0} | all-to-all | bytes 1048576 | tf_op jit(solution)/shard_map/all_to_all | solution.py:127
  (79 shorter events, 18.3 us)
Async XLA Ops:
  6.5 70.9 %all-gather.7.cloned.1.call-start = ((), (), s32[]{:S(2)}) async-start(), calls=%async_computation.2 | async-start | bytes 1671168 | tf_op jit(solution)/shard_map/all_gather | solution.py:47
  8.9 151.4 %all-gather.9.cloned.1.call-start = ((), (), s32[]{:S(2)}) async-start(), calls=%async_computation.3 | async-start | bytes 7864320 | tf_op jit(solution)/shard_map/all_gather | solution.py:48
  80.2 119.9 %all-gather.11.cloned.1.call-start = ((), (), s32[]{:S(2)}) async-start(), calls=%async_computation.4 | async-start | bytes 18874368 | tf_op jit(solution)/shard_map/all_gather | solution.py:49
  160.3 1.0 copy-start
  161.3 6.1 %copy-start.14 = (s32[8]{0:T(128)S(1)}, s32[8]{0:T(128)}, u32[]{:S(2)}) copy-start(s32[8]{0:T(128)} %param.9) | copy-start | bytes 100
  161.3 6.2 %copy-start.13 = (s32[16]{0:T(128)S(1)}, s32[16]{0:T(128)}, u32[]{:S(2)}) copy-start(s32[16]{0:T(128)} %param.8) | copy-start | bytes 196
  162.1 5.5 %collective-permute-start = (bf16[8,1,1024]{2,1,0:T(2,128)(2,1)S(1)}, bf16[8,1,1024]{2,1,0:T(2,128)(2,1)S(1)}, u32[]{:S(2)}, u32[]{:S(2)}) collective-permute-start(bf16[8,1,1024]{2,1,0:T(2,128)(2,1)S(1)} %get-tuple-element.32), channel_id=1, source_target_pairs={{0,1},{1,2},{2,3},{4,5},{5,6},{6,7},{8,9},{9,10},{10,11},{12,13},{... | collective-permute-start | bytes 49160 | tf_op jit(solution)/shard_map/ppermute | solution.py:21
  165.5 5.2 %collective-permute-start.1 = (bf16[8,1,1024]{2,1,0:T(2,128)(2,1)S(1)}, bf16[8,1,1024]{2,1,0:T(2,128)(2,1)S(1)}, u32[]{:S(2)}, u32[]{:S(2)}) collective-permute-start(bf16[8,1,1024]{2,1,0:T(2,128)(2,1)S(1)} %get-tuple-element.33), channel_id=1, source_target_pairs={{1,0},{2,1},{3,2},{5,4},{6,5},{7,6},{9,8},{10,9},{11,10},{13,12},{... | collective-permute-start | bytes 49160 | tf_op jit(solution)/shard_map/ppermute | solution.py:23
  171.0 5.2 %collective-permute-start.2 = (bf16[1,34,1024]{2,1,0:T(8,128)(2,1)S(1)}, bf16[1,34,1024]{2,1,0:T(8,128)(2,1)S(1)}, u32[]{:S(2)}, u32[]{:S(2)}) collective-permute-start(bf16[1,34,1024]{2,1,0:T(8,128)(2,1)S(1)} %slice_select_fusion), channel_id=1, source_target_pairs={{0,4},{4,0},{8,12},{12,8},{16,20},{20,16},{24,28},{28,24},{32,36},... | collective-permute-start | bytes 208904 | tf_op jit(solution)/shard_map/ppermute | solution.py:33
  226.7 1.0 copy-start.9
  226.8 1.4 copy-start.8
  228.2 1.0 copy-start.7
  229.2 1.0 copy-start.6
  230.2 1.0 copy-start.5
  231.3 1.0 copy-start.4
  232.3 1.0 copy-start.3
  233.4 1.0 copy-start.2
  234.4 1.0 copy-start.12
  236.7 35.8 %all-to-all-start = ((bf16[1,32,8,512]{3,2,0,1:T(8,128)(2,1)}), bf16[1,32,8,512]{3,2,0,1:T(8,128)(2,1)S(1)}, u32[]{:S(2)}, u32[]{:S(2)}) async-start(bf16[1,32,8,512]{3,2,0,1:T(8,128)(2,1)} %fusion.18), calls=%async_computation | async-start | bytes 524288 | tf_op jit(solution)/shard_map/all_to_all | solution.py:104
  287.8 1.0 copy-start.11
  288.8 0.9 copy-start.10
  289.7 42.8 %copy-start.1 = (bf16[8,32,1024]{2,1,0:T(8,128)(2,1)S(1)}, bf16[8,32,1024]{2,1,0:T(8,128)(2,1)}, u32[]{:S(2)}) copy-start(bf16[8,32,1024]{2,1,0:T(8,128)(2,1)} %param.5) | copy-start | bytes 1572868
Sparse Core Ops, SparseCore 0:
  9.4 67.9 all-gather.6
  80.3 79.9 all-gather.8
  162.4 37.5 all-gather.10

commit v2 on v0

v2 whole, which is shorter than its diff:
```python
import jax
import jax.numpy as jnp
from jax import lax
from jax.sharding import PartitionSpec as P

DGROUPS = 8
FRAMES = 16
ROWS = 16
ST = ("xhi", "zhi", "zlo")
FS = ("xlo", "core")
FRAME_AXES = ("xhi", "zhi")
ALL = ("xhi", "zhi", "zlo", "xlo", "core")


def padded_2(cells, sides, width):
    for axis, dim in sides:
        count = lax.axis_size(axis)
        ends = count - 1
        head = lax.slice_in_dim(cells, 0, width, axis=dim)
        tail = lax.slice_in_dim(cells, cells.shape[dim] - width, cells.shape[dim], axis=dim)
        cells = jnp.concatenate(
            [
                lax.ppermute(tail, axis, [(i, (i + 1) % count) for i in range(ends)]),
                cells,
                lax.ppermute(head, axis, [((i + 1) % count, i) for i in range(ends)]),
            ],
            axis=dim,
        )
    return cells


def partner(value, axis, distance):
    mask = 2**distance
    pairs = [(source, source ^ mask) for source in range(lax.axis_size(axis))]
    return lax.ppermute(value, axis, pairs)


def gathered_weights(w_spatial, w_temporal):
    flat = jnp.concatenate([w_spatial.reshape(-1), w_temporal.transpose(2, 0, 1).reshape(-1)])
    whole = lax.all_gather(flat, ("zhi", "zlo"), axis=0)
    whole = lax.all_gather(whole, ("xhi", "xlo"), axis=0)
    whole = lax.all_gather(whole, "core", axis=0)
    whole = whole.reshape(-1, flat.shape[0])
    cut = w_spatial.size
    spatial = whole[:, :cut].reshape(-1, w_spatial.shape[2])
    temporal = whole[:, cut:].reshape(-1, w_temporal.shape[0] * w_temporal.shape[1])
    return spatial, temporal


def channel_dims():
    return (
        lax.axis_size("xhi"),
        lax.axis_size("zhi") * lax.axis_size("zlo"),
        lax.axis_size("xlo"),
        lax.axis_size("core"),
    )


def to_gathered_order(cells, block):
    lead = cells.shape[:-1]
    n = len(lead)
    split = cells.reshape(lead + channel_dims() + (block,))
    order = tuple(range(n)) + (n + 3, n, n + 2, n + 1, n + 4)
    return split.transpose(order).reshape(lead + (-1, block))


def from_gathered_order(cells, block):
    lead = cells.shape[:-1]
    n = len(lead)
    xhi, z, xlo, core = channel_dims()
    split = cells.reshape(lead + (core, xhi, xlo, z, block))
    order = tuple(range(n)) + (n + 1, n + 3, n + 2, n, n + 4)
    return split.transpose(order).reshape(lead + (-1,))


def shards(clip_tokens, w_spatial, w_temporal, frame_time, dilation):
    rows_dev, cols_dev, channels = clip_tokens.shape
    middle = w_spatial.shape[2]
    block_in = w_spatial.shape[1]
    block_out = w_temporal.shape[2]
    spatial_w, temporal_w = gathered_weights(w_spatial, w_temporal)
    values = clip_tokens.astype(jnp.float32)
    average = jnp.mean(values, axis=-1, keepdims=True)
    kernel_extent = jnp.mean(jnp.square(values - average), axis=-1, keepdims=True)
    normed = ((values - average) * lax.rsqrt(kernel_extent + 1e-06)).astype(jnp.bfloat16)
    normed = to_gathered_order(normed, block_in).reshape(rows_dev, cols_dev, channels)
    widened = padded_2(normed, ((FS, 1),), 1)
    blank_row = jnp.zeros((1,) + widened.shape[1:], jnp.bfloat16)
    lower_half = lax.axis_index(ST) % 2 == 1
    outgoing = jnp.where(lower_half, widened[:1], widened[-1:])
    incoming = partner(outgoing, ST, 0)
    top_rim = jnp.where(lower_half, incoming, blank_row)
    bottom_rim = jnp.where(lower_half, blank_row, incoming)
    padded = jnp.concatenate([top_rim, widened, bottom_rim], axis=0)
    first_row = lax.axis_index(ST) * rows_dev
    in_frame = (first_row + jnp.arange(rows_dev, dtype=jnp.int32)) % ROWS
    windows = []
    for shift_amount in (-1, 0, 1):
        inside = ((in_frame + shift_amount >= 0) & (in_frame + shift_amount < ROWS)).astype(
            jnp.bfloat16
        )
        windows.append(
            padded[1 + shift_amount : 1 + shift_amount + rows_dev] * inside[:, None, None]
        )
    tokens = rows_dev * cols_dev
    taps = []
    for row_tap in range(3):
        for column_kernel_tap in range(3):
            patches = windows[row_tap][:, column_kernel_tap : column_kernel_tap + cols_dev, :]
            taps.append(patches.reshape(tokens, -1, block_in))
    im2col = jnp.stack(taps, axis=2).reshape(tokens, -1)
    running = jnp.dot(im2col, spatial_w, preferred_element_type=jnp.float32)
    hidden = jax.nn.gelu(running).astype(jnp.bfloat16)
    group_size = lax.axis_size(FRAME_AXES)
    per_pixel = tokens // group_size
    arrived = lax.all_to_all(
        hidden.reshape(group_size, per_pixel, middle), FRAME_AXES, 0, 0, tiled=True
    )
    group_width = middle // DGROUPS
    frame_sequence = arrived.reshape(FRAMES, per_pixel, DGROUPS, group_width)
    offsets = (jnp.arange(3, dtype=jnp.int32) - 1)[None, :] * dilation[:, None]
    selector_matrix = (
        frame_time[None, None, None, :]
        == frame_time[None, None, :, None] + offsets[:, :, None, None]
    ).astype(jnp.bfloat16)
    stacked_panels = jnp.einsum(
        "gkfe,epgc->fpkgc", selector_matrix, frame_sequence, preferred_element_type=jnp.float32
    )
    stacked_panels = stacked_panels.astype(jnp.bfloat16).reshape(FRAMES * per_pixel, -1)
    result = lax.dot_general(
        stacked_panels, temporal_w, (((1,), (1,)), ((), ())), preferred_element_type=jnp.float32
    )
    mixed_out = from_gathered_order(result.astype(jnp.bfloat16), block_out)
    returned = lax.all_to_all(
        mixed_out.reshape(group_size, per_pixel, channels), FRAME_AXES, 0, 0, tiled=True
    )
    update = returned.reshape(rows_dev, cols_dev, channels)
    return (values + update.astype(jnp.float32)).astype(jnp.bfloat16)


def solution(mesh):
    clips = mesh.shape["clip"]
    fine = jax.sharding.Mesh(
        mesh.devices.reshape(clips, 2, -1, 2, 2, 2), ("clip",) + ALL
    )
    return jax.shard_map(
        shards,
        mesh=fine,
        in_specs=(
            P(("clip",) + ST, FS, None),
            P(None, ALL, None),
            P(None, None, ALL),
            P("clip"),
            P("clip"),
        ),
        out_specs=P(("clip",) + ST, FS, None),
        check_vma=False,
    )
```

time: 524 us -> 372 us (0.71)
  waiting for transfers between devices: 417 us -> 159 us
  local copies, waits for them, and re-layouts: 5.82 us -> 115 us
    all_gather x2 -> x3, waiting for transfers between devices: 391 us -> 148 us  [the longest x1 80.1 us: gathered_weights(): whole = lax.all_gather(whole, ('xhi', 'xlo'), axis=0)]
    another operation x0 -> x13, local copies, waits for them, and re-layouts: none -> 30.7 us  [the longest x11 22.2 us: shards(): im2col = jnp.stack(taps, axis=2).reshape(tokens, -1)]
    slice x3 -> x12, local copies, waits for them, and re-layouts: 2.62 us -> 28 us  [shards(): windows[row_tap][:, column_kernel_tap:column_kernel_tap + cols_dev, :]]
    reshape x0 -> x4, local copies, waits for them, and re-layouts: none -> 18.1 us  [the longest x1 14.1 us: gathered_weights(): spatial = whole[:, :cut].reshape(-1, w_spatial.shape[2])]
    slice x4 -> x3, local copies, waits for them, and re-layouts: 1.3 us -> 12.2 us  [the longest x1 8.14 us: gathered_weights(): spatial = whole[:, :cut].reshape(-1, w_spatial.shape[2])]
    all_to_all x1, waiting for transfers between devices: 20.3 us -> 9.56 us  [shards(): lax.all_to_all(hidden.reshape(group_size, per_pixel, middle), FRAME_AXES,...]
    unnamed x12 -> x37, local copies, waits for them, and re-layouts: 0.61 us -> 6.98 us
    dot_general x13 -> x3, matrix products: 16.7 us -> 12.3 us  [the longest x1 8.56 us: shards(): running = jnp.dot(im2col, spatial_w, preferred_element_type=jnp.float32)]
  transfers between devices with their start and end apart: 6 -> 7, of which waited for: 5 -> 4; matrix products, arithmetic and copies ran while one was open for 4% -> 22% of each run, Pallas kernels for 0% -> 0%
where the time goes in v2:
time: 372 us; the launch traced here: 367 us
  waiting for transfers between devices  159 us (43%)
  local copies, waits for them, and re-layouts  115 us (31%)
  blocking collectives  37.3 us (10%)
  starting transfers between devices  21.9 us (6%)
  between operations  13.5 us (4%)
  matrix products  12.3 us (3%)
  other arithmetic  8.32 us (2%)
    all_gather x1, waiting for transfers between devices, gathered_weights(): whole = lax.all_gather(whole, ('xhi', 'xlo'), axis=0)  80.1 us
    all_gather x1, waiting for transfers between devices, gathered_weights(): whole = lax.all_gather(flat, ('zhi', 'zlo'), axis=0)  68.4 us
    all_to_all x1, blocking collectives, shards(): lax.all_to_all(mixed_out.reshape(group_size, per_pixel, channels), FRAME_...  37.3 us
    slice x12, local copies, waits for them, and re-layouts, shards(): windows[row_tap][:, column_kernel_tap:column_kernel_tap + cols_dev, :]  28 us
    another operation x11, local copies, waits for them, and re-layouts, shards(): im2col = jnp.stack(taps, axis=2).reshape(tokens, -1)  22.2 us
    reshape x1, local copies, waits for them, and re-layouts, gathered_weights(): spatial = whole[:, :cut].reshape(-1, w_spatial.shape[2])  14.1 us
    all_to_all x1, starting transfers between devices, shards(): lax.all_to_all(hidden.reshape(group_size, per_pixel, middle), FRAME_AXES,...  13 us
    all_to_all x1, waiting for transfers between devices, shards(): lax.all_to_all(hidden.reshape(group_size, per_pixel, middle), FRAME_AXES,...  9.56 us
  transfers between devices with their start and end apart: 7, of which 4 were waited for; matrix products, arithmetic and copies ran while one was open for 22% of the time, Pallas kernels for 0%

profile of v2, /device:TPU:1, one launch (start us, length us, event | category | flops | bytes accessed | tf_op | source)
XLA Modules:
  0.0 367.0 jit_solution(8084138132875878886)
XLA Ops:
  9.0 68.4 %all-gather.7.cloned.1.call-done = bf16[786432]{0:T(1024)(128)(2,1)} async-done(((bf16[49152]{0:T(1024)(128)(2,1)}), bf16[786432]{0:T(1024)(128)(2,1)}) %all-gather.7.cloned.1.call-update) | async-done | bytes 1572880 | tf_op jit(solution)/shard_map/all_gather | solution.py:40
  77.4 2.8 reshape.133
  80.2 80.1 %all-gather.9.cloned.1.call-done = bf16[64,49152]{1,0:T(8,128)(2,1)} async-done(((bf16[16,49152]{1,0:T(8,128)(2,1)}), bf16[64,49152]{1,0:T(8,128)(2,1)}) %all-gather.9.cloned.1.call-update) | async-done | bytes 6291472 | tf_op jit(solution)/shard_map/all_gather | solution.py:41
  165.9 2.8 fusion.23
  170.7 2.6 collective-permute-start.1
  175.3 2.9 collective-permute-start
  182.8 5.6 %broadcast_multiply_fusion = (bf16[8,34,1024]{1,2,0:T(8,128)(2,1)S(1)}, bf16[8,34,1024]{1,2,0:T(8,128)(2,1)S(1)}) fusion(bf16[8]{0:T(256)(128)(2,1)S(1)} %and_convert_fusion.1, bf16[8,1,1024]{1,2,0:T(8,128)(2,1)} %copy.104, bf16[8,32,1024]{1,2,0:T(8,128)(2,1)S(1)} %bitcast.55, bf16[8,1,1024]{1,2,0:T(8,128)(2,1)} %copy.103), kind=kLoop, calls=%fused_computation.12 | loop fusion | flops 2506752 | bytes 1671184 | tf_op jit(solution)/shard_map/mul | solution.py:103
  189.8 3.3 collective-permute-start.2
  193.1 4.0 %fusion.22 = (bf16[8,32,1024]{1,2,0:T(8,128)(2,1)}, bf16[8,32,1024]{1,2,0:T(8,128)(2,1)}, bf16[8,32,1024]{1,2,0:T(8,128)(2,1)}) fusion(bf16[8,34,1024]{1,2,0:T(8,128)(2,1)S(1)} %get-tuple-element.5), kind=kLoop, calls=%fused_computation.56 | loop fusion | bytes 3145728 | tf_op jit(solution)/shard_map/slice | solution.py:109
  198.0 2.9 copy.112
  201.0 2.2 stack_reshape.32
  203.1 2.9 copy.111
  206.1 2.2 stack_reshape.31
  208.3 2.9 copy.110
  215.2 2.5 copy.117
  217.8 2.2 stack_reshape.35
  221.2 2.6 copy.109
  227.6 2.2 stack_reshape.28
  229.8 2.6 copy.107
  232.4 2.4 stack_reshape.27
  236.4 2.2 stack_reshape.34
  246.2 2.4 copy.118
  248.6 8.1 %slice.83 = bf16[128,36864]{1,0:T(8,128)(2,1)} slice(bf16[128,49152]{1,0:T(8,128)(2,1)} %bitcast.57), slice={[0:128], [0:36864]} | slice | bytes 18874368 | tf_op jit(solution)/shard_map/slice | solution.py:45
  256.8 14.1 %reshape.126 = bf16[9216,512]{1,0:T(8,128)(2,1)} reshape(bf16[128,36864]{1,0:T(8,128)(2,1)} %slice.83) | data formatting | bytes 18874368 | tf_op jit(solution)/shard_map/reshape | solution.py:45
  270.9 8.6 %fusion.15 = bf16[256,512]{1,0:T(8,128)(2,1)} fusion(bf16[256,9216]{0,1:T(8,128)(2,1)} %bitcast.56, bf16[9216,512]{1,0:T(8,128)(2,1)} %reshape.126), kind=kOutput, calls=%fused_computation.25 | convolution fusion | flops 2417098752 | bytes 14417920 | tf_op jit(solution)/shard_map/dot_general | solution.py:112
  279.5 13.0 %all-to-all-start = ((bf16[16,16,512]{2,1,0:T(8,128)(2,1)}), bf16[16,16,512]{2,1,0:T(8,128)(2,1)S(1)}, u32[]{:S(2)}, u32[]{:S(2)}) async-start(bf16[16,16,512]{2,1,0:T(8,128)(2,1)} %bitcast.7), calls=%async_computation | async-start | bytes 524288 | tf_op jit(solution)/shard_map/all_to_all | solution.py:116
  294.7 2.9 reshape.130
  297.7 9.6 %all-to-all-done = bf16[16,16,512]{2,1,0:T(8,128)(2,1)S(1)} async-done(((bf16[16,16,512]{2,1,0:T(8,128)(2,1)}), bf16[16,16,512]{2,1,0:T(8,128)(2,1)S(1)}, u32[]{:S(2)}, u32[]{:S(2)}) %all-to-all-start) | async-done | bytes 262176 | tf_op jit(solution)/shard_map/all_to_all | solution.py:116
  310.4 2.9 convolution_convert_fusion.1
  313.6 4.1 %reshape_reshape.7 = bf16[16,16,1024]{1,0,2:T(8,128)(2,1)} reshape(bf16[256,2,16,2,2,8]{0,5,4,3,2,1:T(8,128)(2,1)S(1)} %copy.123) | data formatting | bytes 1048576 | tf_op jit(solution)/shard_map/reshape;reshape | solution.py:135
  317.6 4.5 %copy.124 = bf16[16,16,1024]{2,1,0:T(8,128)(2,1)S(1)} copy(bf16[16,16,1024]{1,0,2:T(8,128)(2,1)} %reshape_reshape.7) | data formatting | bytes 1048576 | tf_op jit(solution)/shard_map/reshape;reshape | solution.py:135
  322.1 37.3 %all_to_all.10 = bf16[16,16,1024]{2,1,0:T(8,128)(2,1)S(1)} all-to-all(bf16[16,16,1024]{2,1,0:T(8,128)(2,1)S(1)} %copy.124), channel_id=1, replica_groups=mesh['clip'=4,'xhi'=2,'zhi'=8,'zlo'=2,'xlo'=2,'core'=2] {'xhi','zhi'}, dimensions={0} | all-to-all | bytes 1048576 | tf_op jit(solution)/shard_map/all_to_all | solution.py:134
  (89 shorter events, 43.7 us)
Async XLA Ops:
  6.5 70.9 %all-gather.7.cloned.1.call-start = ((), (), s32[]{:S(2)}) async-start(), calls=%async_computation.2 | async-start | bytes 1671168 | tf_op jit(solution)/shard_map/all_gather | solution.py:40
  8.9 151.4 %all-gather.9.cloned.1.call-start = ((), (), s32[]{:S(2)}) async-start(), calls=%async_computation.3 | async-start | bytes 7864320 | tf_op jit(solution)/shard_map/all_gather | solution.py:41
  80.2 168.5 %all-gather.11.cloned.1.call-start = ((), (), s32[]{:S(2)}) async-start(), calls=%async_computation.4 | async-start | bytes 18874368 | tf_op jit(solution)/shard_map/all_gather | solution.py:42
  160.3 1.0 copy-start.2
  170.7 10.3 %collective-permute-start.1 = (bf16[8,1,1024]{2,0,1:T(8,128)(2,1)S(1)}, bf16[8,1,1024]{2,0,1:T(8,128)(2,1)S(1)}, u32[]{:S(2)}, u32[]{:S(2)}) collective-permute-start(bf16[8,1,1024]{2,0,1:T(8,128)(2,1)S(1)} %copy.102), channel_id=1, source_target_pairs={{1,0},{2,1},{3,2},{5,4},{6,5},{7,6},{9,8},{10,9},{11,10},{13,12},{... | collective-permute-start | bytes 49160 | tf_op jit(solution)/shard_map/ppermute | solution.py:25
  175.3 3.8 %collective-permute-start = (bf16[8,1,1024]{2,0,1:T(8,128)(2,1)S(1)}, bf16[8,1,1024]{2,0,1:T(8,128)(2,1)S(1)}, u32[]{:S(2)}, u32[]{:S(2)}) collective-permute-start(bf16[8,1,1024]{2,0,1:T(8,128)(2,1)S(1)} %copy.101), channel_id=1, source_target_pairs={{0,1},{1,2},{2,3},{4,5},{5,6},{6,7},{8,9},{9,10},{10,11},{12,13},{... | collective-permute-start | bytes 49160 | tf_op jit(solution)/shard_map/ppermute | solution.py:23
  188.3 1.4 copy-start
  189.8 23.6 %collective-permute-start.2 = (bf16[1,34,1024]{1,2,0:T(8,128)(2,1)S(1)}, bf16[1,34,1024]{1,2,0:T(8,128)(2,1)S(1)}, u32[]{:S(2)}, u32[]{:S(2)}) collective-permute-start(bf16[1,34,1024]{1,2,0:T(8,128)(2,1)S(1)} %slice_select_fusion), channel_id=1, source_target_pairs={{0,4},{4,0},{8,12},{12,8},{16,20},{20,16},{24,28},{28,24},{32,36},... | collective-permute-start | bytes 208904 | tf_op jit(solution)/shard_map/ppermute | solution.py:35
  193.0 4.0 %copy-start.1 = (bf16[8,34,1024]{1,2,0:T(8,128)(2,1)S(1)}, bf16[8,34,1024]{1,2,0:T(8,128)(2,1)}, u32[]{:S(2)}) copy-start(bf16[8,34,1024]{1,2,0:T(8,128)(2,1)} %copy-done) | copy-start | bytes 1671172
  221.2 4.8 %copy-start.11 = (bf16[8,32,1024]{2,1,0:T(8,128)(2,1)S(1)}, bf16[8,32,1024]{2,1,0:T(8,128)(2,1)}, u32[]{:S(2)}) copy-start(bf16[8,32,1024]{2,1,0:T(8,128)(2,1)} %get-tuple-element.18) | copy-start | bytes 1572868
  229.8 5.0 %copy-start.10 = (bf16[8,32,1024]{2,1,0:T(8,128)(2,1)S(1)}, bf16[8,32,1024]{2,1,0:T(8,128)(2,1)}, u32[]{:S(2)}) copy-start(bf16[8,32,1024]{2,1,0:T(8,128)(2,1)} %get-tuple-element.13) | copy-start | bytes 1572868
  240.2 5.6 %copy-start.6 = (bf16[256,128,1,8]{0,3,1,2:T(8,128)(2,1)S(1)}, bf16[256,128,1,8]{0,3,1,2:T(8,128)(2,1)}, u32[]{:S(2)}) copy-start(bf16[256,128,1,8]{0,3,1,2:T(8,128)(2,1)} %stack_reshape.30) | copy-start | bytes 1572868
  240.2 5.7 %copy-start.5 = (bf16[256,128,1,8]{0,3,1,2:T(8,128)(2,1)S(1)}, bf16[256,128,1,8]{0,3,1,2:T(8,128)(2,1)}, u32[]{:S(2)}) copy-start(bf16[256,128,1,8]{0,3,1,2:T(8,128)(2,1)} %stack_reshape.31) | copy-start | bytes 1572868
  242.4 3.6 copy-start.4
  242.4 3.6 copy-start.9
  243.6 2.5 copy-start.8
  244.7 1.4 copy-start.7
  270.9 21.6 %copy-start.13 = (s32[8]{0:T(128)S(1)}, s32[8]{0:T(128)}, u32[]{:S(2)}) copy-start(s32[8]{0:T(128)} %param.9) | copy-start | bytes 100
  270.9 21.7 %copy-start.12 = (s32[16]{0:T(128)S(1)}, s32[16]{0:T(128)}, u32[]{:S(2)}) copy-start(s32[16]{0:T(128)} %param.8) | copy-start | bytes 196
  279.5 27.8 %all-to-all-start = ((bf16[16,16,512]{2,1,0:T(8,128)(2,1)}), bf16[16,16,512]{2,1,0:T(8,128)(2,1)S(1)}, u32[]{:S(2)}, u32[]{:S(2)}) async-start(bf16[16,16,512]{2,1,0:T(8,128)(2,1)} %bitcast.7), calls=%async_computation | async-start | bytes 524288 | tf_op jit(solution)/shard_map/all_to_all | solution.py:116
  317.6 41.8 %copy-start.3 = (bf16[8,32,1024]{2,1,0:T(8,128)(2,1)S(1)}, bf16[8,32,1024]{2,1,0:T(8,128)(2,1)}, u32[]{:S(2)}) copy-start(bf16[8,32,1024]{2,1,0:T(8,128)(2,1)} %param.5) | copy-start | bytes 1572868
Sparse Core Ops, SparseCore 0:
  9.4 67.9 all-gather.6
  80.3 79.9 all-gather.8
  162.4 37.5 all-gather.10

commit v3 on v2

--- a/solution.py
+++ b/solution.py
@@ -35,16 +35,11 @@
     return lax.ppermute(value, axis, pairs)
 
 
-def gathered_weights(w_spatial, w_temporal):
-    flat = jnp.concatenate([w_spatial.reshape(-1), w_temporal.transpose(2, 0, 1).reshape(-1)])
-    whole = lax.all_gather(flat, ("zhi", "zlo"), axis=0)
-    whole = lax.all_gather(whole, ("xhi", "xlo"), axis=0)
-    whole = lax.all_gather(whole, "core", axis=0)
-    whole = whole.reshape(-1, flat.shape[0])
-    cut = w_spatial.size
-    spatial = whole[:, :cut].reshape(-1, w_spatial.shape[2])
-    temporal = whole[:, cut:].reshape(-1, w_temporal.shape[0] * w_temporal.shape[1])
-    return spatial, temporal
+def weight_rows(w_spatial, w_temporal):
+    middle = w_spatial.shape[2]
+    return jnp.concatenate(
+        [w_spatial.reshape(-1, middle), w_temporal.transpose(2, 0, 1).reshape(-1, middle)], axis=0
+    )
 
 
 def channel_dims():
@@ -78,7 +73,8 @@
     middle = w_spatial.shape[2]
     block_in = w_spatial.shape[1]
     block_out = w_temporal.shape[2]
-    spatial_w, temporal_w = gathered_weights(w_spatial, w_temporal)
+    spatial_rows = w_spatial.shape[0] * block_in
+    along_z = lax.all_gather(weight_rows(w_spatial, w_temporal), ("zhi", "zlo"), axis=0)
     values = clip_tokens.astype(jnp.float32)
     average = jnp.mean(values, axis=-1, keepdims=True)
     kernel_extent = jnp.mean(jnp.square(values - average), axis=-1, keepdims=True)
@@ -108,8 +104,16 @@
         for column_kernel_tap in range(3):
             patches = windows[row_tap][:, column_kernel_tap : column_kernel_tap + cols_dev, :]
             taps.append(patches.reshape(tokens, -1, block_in))
-    im2col = jnp.stack(taps, axis=2).reshape(tokens, -1)
-    running = jnp.dot(im2col, spatial_w, preferred_element_type=jnp.float32)
+    im2col = jnp.stack(taps, axis=2).reshape(tokens, -1, spatial_rows)
+    pad_rows = along_z.shape[1] - spatial_rows
+    im2col = jnp.pad(im2col, ((0, 0), (0, 0), (0, pad_rows)))
+    along_z, im2col = lax.optimization_barrier((along_z, im2col))
+    whole = lax.all_gather(along_z, ("xhi", "xlo"), axis=0)
+    whole = lax.all_gather(whole, "core", axis=0)
+    whole = whole.reshape((-1,) + along_z.shape[1:])
+    running = lax.dot_general(
+        im2col, whole, (((1, 2), (0, 1)), ((), ())), preferred_element_type=jnp.float32
+    )
     hidden = jax.nn.gelu(running).astype(jnp.bfloat16)
     group_size = lax.axis_size(FRAME_AXES)
     per_pixel = tokens // group_size
@@ -126,10 +130,12 @@
     stacked_panels = jnp.einsum(
         "gkfe,epgc->fpkgc", selector_matrix, frame_sequence, preferred_element_type=jnp.float32
     )
-    stacked_panels = stacked_panels.astype(jnp.bfloat16).reshape(FRAMES * per_pixel, -1)
+    stacked_panels = stacked_panels.astype(jnp.bfloat16).reshape(FRAMES * per_pixel, 3, middle)
+    temporal_w = whole[:, spatial_rows:, :].reshape(whole.shape[0], block_out, 3, middle)
     result = lax.dot_general(
-        stacked_panels, temporal_w, (((1,), (1,)), ((), ())), preferred_element_type=jnp.float32
+        stacked_panels, temporal_w, (((1, 2), (2, 3)), ((), ())), preferred_element_type=jnp.float32
     )
+    result = result.reshape(FRAMES * per_pixel, channels)
     mixed_out = from_gathered_order(result.astype(jnp.bfloat16), block_out)
     returned = lax.all_to_all(
         mixed_out.reshape(group_size, per_pixel, channels), FRAME_AXES, 0, 0, tiled=True

time: 372 us -> 341 us (0.917); the launches traced: 367 us -> 340 us
  waiting for transfers between devices: 159 us -> 121 us
  starting transfers between devices: 21.9 us -> 26.1 us
    all_gather x3, waiting for transfers between devices: 148 us -> 114 us  [the longest x1 74 us: shards(): whole = lax.all_gather(along_z, ('xhi', 'xlo'), axis=0)]
    reshape x4 -> x2, local copies, waits for them, and re-layouts: 18.1 us -> 0.99 us  [the longest x1 0.96 us: shards(): stacked_panels.astype(jnp.bfloat16).reshape(FRAMES * per_pixel, 3, middle)]
    slice x2, local copies, waits for them, and re-layouts: 10.2 us -> 3.94 us  [shards(): whole[:, spatial_rows:, :].reshape(whole.shape[0], block_out, 3, middle)]
    ppermute x1, starting transfers between devices: 2.62 us -> 8.79 us  [padded_2(): lax.ppermute(head, axis, [((i + 1) % count, i) for i in range(ends)])]
    pad x0 -> x1, local copies, waits for them, and re-layouts: none -> 5.93 us  [shards(): im2col = jnp.pad(im2col, ((0, 0), (0, 0), (0, pad_rows)))]
    another operation x11, local copies, waits for them, and re-layouts: 22.2 us -> 27.9 us  [shards(): im2col = jnp.stack(taps, axis=2).reshape(tokens, -1, spatial_rows)]
    unnamed x37 -> x30, local copies, waits for them, and re-layouts: 6.98 us -> 11.3 us
    dot_general x0 -> x1, local copies, waits for them, and re-layouts: none -> 4.3 us  [shards(): lax.dot_general(stacked_panels, temporal_w, (((1, 2), (2, 3)), ((), ())),...]
  transfers between devices with their start and end apart: 7 -> 7, of which waited for: 4 -> 3; matrix products, arithmetic and copies ran while one was open for 22% -> 31% of each run, Pallas kernels for 0% -> 0%
where the time goes in v3:
time: 341 us; the launch traced here: 340 us
  waiting for transfers between devices  121 us (35%)
  local copies, waits for them, and re-layouts  113 us (33%)
  blocking collectives  40.9 us (12%)
  starting transfers between devices  26.1 us (8%)
  matrix products  13.8 us (4%)
  between operations  13.4 us (4%)
  other arithmetic  11.2 us (3%)
    all_gather x1, waiting for transfers between devices, shards(): whole = lax.all_gather(along_z, ('xhi', 'xlo'), axis=0)  74 us
    all_to_all x1, blocking collectives, shards(): lax.all_to_all(mixed_out.reshape(group_size, per_pixel, channels), FRAME_...  40.9 us
    all_gather x1, waiting for transfers between devices, shards(): whole = lax.all_gather(whole, 'core', axis=0)  39.7 us
    slice x12, local copies, waits for them, and re-layouts, shards(): windows[row_tap][:, column_kernel_tap:column_kernel_tap + cols_dev, :]  28.8 us
    another operation x11, local copies, waits for them, and re-layouts, shards(): im2col = jnp.stack(taps, axis=2).reshape(tokens, -1, spatial_rows)  27.9 us
    all_to_all x1, starting transfers between devices, shards(): lax.all_to_all(hidden.reshape(group_size, per_pixel, middle), FRAME_AXES,...  13.4 us
    unnamed x30, local copies, waits for them, and re-layouts  11.3 us
    dot_general x1, matrix products, shards(): lax.dot_general(im2col, whole, (((1, 2), (0, 1)), ((), ())), preferred_el...  9.53 us
  transfers between devices with their start and end apart: 7, of which 3 were waited for; matrix products, arithmetic and copies ran while one was open for 31% of the time, Pallas kernels for 0%

profile of v3, /device:TPU:1, one launch (start us, length us, event | category | flops | bytes accessed | tf_op | source)
XLA Modules:
  0.0 339.7 jit_solution(13393715489376094086)
XLA Ops:
  16.7 2.7 fusion.40
  21.3 8.8 %collective-permute-start.1 = (bf16[8,1,1024]{2,0,1:T(8,128)(2,1)S(1)}, bf16[8,1,1024]{2,0,1:T(8,128)(2,1)S(1)}, u32[]{:S(2)}, u32[]{:S(2)}) collective-permute-start(bf16[8,1,1024]{2,0,1:T(8,128)(2,1)S(1)} %copy.118), channel_id=1, source_target_pairs={{1,0},{2,1},{3,2},{5,4},{6,5},{7,6},{9,8},{10,9},{11,10},{13,12},{... | collective-permute-start | bytes 49160 | tf_op jit(solution)/shard_map/ppermute | solution.py:25
  37.8 4.4 %broadcast_multiply_fusion = (bf16[8,34,1024]{1,2,0:T(8,128)(2,1)S(1)}, bf16[8,34,1024]{1,2,0:T(8,128)(2,1)S(1)}) fusion(bf16[8]{0:T(256)(128)(2,1)S(1)} %and_convert_fusion.1, bf16[8,1,1024]{1,2,0:T(8,128)(2,1)} %copy.120, bf16[8,32,1024]{1,2,0:T(8,128)(2,1)S(1)} %bitcast.65, bf16[8,1,1024]{1,2,0:T(8,128)(2,1)} %copy.119), kind=kLoop, calls=%fused_computation.18 | loop fusion | flops 2506752 | bytes 1671184 | tf_op jit(solution)/shard_map/mul | solution.py:99
  45.5 3.9 %fusion.39 = (bf16[8,32,1024]{1,2,0:T(8,128)(2,1)}, bf16[8,32,1024]{1,2,0:T(8,128)(2,1)}, bf16[8,32,1024]{1,2,0:T(8,128)(2,1)}) fusion(bf16[8,34,1024]{1,2,0:T(8,128)(2,1)S(1)} %get-tuple-element.9), kind=kLoop, calls=%fused_computation.62 | loop fusion | bytes 3145728 | tf_op jit(solution)/shard_map/slice | solution.py:105
  50.4 3.0 copy.126
  55.5 2.9 copy.127
  58.5 2.2 stack_reshape.31
  60.6 3.0 copy.128
  63.6 2.2 stack_reshape.32
  67.5 2.5 copy.123
  70.1 2.2 stack_reshape.27
  72.3 2.5 copy.124
  74.8 2.2 stack_reshape.28
  78.6 2.2 stack_reshape.29
  82.0 2.5 copy.131
  84.6 2.4 stack_reshape.33
  90.7 2.6 copy.133
  93.4 2.2 stack_reshape.35
  106.3 7.4 %copy.134 = bf16[256,128,9,8]{1,3,2,0:T(8,128)(2,1)} copy(bf16[256,128,9,8]{0,3,1,2:T(8,128)(2,1)} %constant_dynamic-update-slice_fusion) | data formatting | bytes 9437184 | tf_op jit(solution)/shard_map/stack | solution.py:107
  113.8 5.9 %pad.4 = bf16[256,128,96]{1,2,0:T(8,128)(2,1)} pad(bf16[256,128,72]{1,2,0:T(8,128)(2,1)} %bitcast.66, bf16[]{:T(256)} %constant.64.clone.1), padding=0_0x0_0x0_24 | pad | bytes 11010050 | tf_op jit(solution)/shard_map/jit(_pad)/pad | solution.py:109
  119.7 3.4 %copy.135 = bf16[16,96,512]{2,0,1:T(8,128)(2,1)} copy(bf16[16,96,512]{2,1,0:T(8,128)(2,1)} %bitcast.72) | data formatting | bytes 3145728 | tf_op jit(solution)/shard_map/optimization_barrier | solution.py:110
  123.2 74.0 %all-gather.9.cloned.1.call-done = bf16[64,96,512]{2,0,1:T(8,128)(2,1)} async-done(((bf16[16,96,512]{2,0,1:T(8,128)(2,1)}), bf16[64,96,512]{2,0,1:T(8,128)(2,1)}) %all-gather.9.cloned.1.call-update) | async-done | bytes 6291472 | tf_op jit(solution)/shard_map/all_gather | solution.py:111
  197.3 39.7 %all-gather.11.cloned.1.call-done = bf16[8,16,96,512]{3,1,0,2:T(8,128)(2,1)} async-done(((bf16[4,16,96,512]{3,1,0,2:T(8,128)(2,1)}), bf16[8,16,96,512]{3,1,0,2:T(8,128)(2,1)}) %all-gather.11.cloned.1.call-update) | async-done | bytes 12582928 | tf_op jit(solution)/shard_map/all_gather | solution.py:112
  237.0 9.5 %fusion.30 = bf16[256,512]{1,0:T(8,128)(2,1)} fusion(bf16[128,96,512]{2,0,1:T(8,128)(2,1)} %bitcast.73, bf16[256,128,96]{1,2,0:T(8,128)(2,1)} %pad.4), kind=kOutput, calls=%fused_computation.31 | convolution fusion | flops 3222405120 | bytes 19136512 | tf_op jit(solution)/shard_map/dot_general | solution.py:114
  246.5 13.4 %all-to-all-start = ((bf16[16,16,512]{2,1,0:T(8,128)(2,1)}), bf16[16,16,512]{2,1,0:T(8,128)(2,1)S(1)}, u32[]{:S(2)}, u32[]{:S(2)}) async-start(bf16[16,16,512]{2,1,0:T(8,128)(2,1)} %bitcast.10), calls=%async_computation | async-start | bytes 524288 | tf_op jit(solution)/shard_map/all_to_all | solution.py:120
  260.1 2.2 slice.79
  264.1 4.3 %dot_general.13 = bf16[1024,3,512]{2,1,0:T(4,128)(2,1)} reshape(bf16[128,24,512]{2,1,0:T(8,128)(2,1)S(1)} %copy.139) | data formatting | bytes 6291456 | tf_op jit(solution)/shard_map/dot_general | solution.py:135
  268.4 7.6 %all-to-all-done = bf16[16,16,512]{2,1,0:T(8,128)(2,1)S(1)} async-done(((bf16[16,16,512]{2,1,0:T(8,128)(2,1)}), bf16[16,16,512]{2,1,0:T(8,128)(2,1)S(1)}, u32[]{:S(2)}, u32[]{:S(2)}) %all-to-all-start) | async-done | bytes 262176 | tf_op jit(solution)/shard_map/all_to_all | solution.py:120
  279.1 3.4 fusion.8
  282.7 4.1 %reshape_reshape.7 = bf16[16,16,1024]{1,0,2:T(8,128)(2,1)} reshape(bf16[256,2,16,2,2,8]{0,5,4,3,2,1:T(8,128)(2,1)S(1)} %copy.142) | data formatting | bytes 1048576 | tf_op jit(solution)/shard_map/reshape;reshape | solution.py:141
  286.8 4.4 %copy.143 = bf16[16,16,1024]{2,1,0:T(8,128)(2,1)S(1)} copy(bf16[16,16,1024]{1,0,2:T(8,128)(2,1)} %reshape_reshape.7) | data formatting | bytes 1048576 | tf_op jit(solution)/shard_map/reshape;reshape | solution.py:141
  291.2 40.9 %all_to_all.10 = bf16[16,16,1024]{2,1,0:T(8,128)(2,1)S(1)} all-to-all(bf16[16,16,1024]{2,1,0:T(8,128)(2,1)S(1)} %copy.143), channel_id=1, replica_groups=mesh['clip'=4,'xhi'=2,'zhi'=8,'zlo'=2,'xlo'=2,'core'=2] {'xhi','zhi'}, dimensions={0} | all-to-all | bytes 1048576 | tf_op jit(solution)/shard_map/all_to_all | solution.py:140
  (82 shorter events, 51.6 us)
Async XLA Ops:
  6.5 113.2 %all-gather.7.cloned.1.call-start = ((), (), s32[]{:S(2)}) async-start(), calls=%async_computation.2 | async-start | bytes 1671168 | tf_op jit(solution)/shard_map/all_gather | solution.py:77
  8.9 188.4 %all-gather.9.cloned.1.call-start = ((), (), s32[]{:S(2)}) async-start(), calls=%async_computation.3 | async-start | bytes 7864320 | tf_op jit(solution)/shard_map/all_gather | solution.py:111
  21.3 12.8 %collective-permute-start.1 = (bf16[8,1,1024]{2,0,1:T(8,128)(2,1)S(1)}, bf16[8,1,1024]{2,0,1:T(8,128)(2,1)S(1)}, u32[]{:S(2)}, u32[]{:S(2)}) collective-permute-start(bf16[8,1,1024]{2,0,1:T(8,128)(2,1)S(1)} %copy.118), channel_id=1, source_target_pairs={{1,0},{2,1},{3,2},{5,4},{6,5},{7,6},{9,8},{10,9},{11,10},{13,12},{... | collective-permute-start | bytes 49160 | tf_op jit(solution)/shard_map/ppermute | solution.py:25
  32.1 3.9 %collective-permute-start = (bf16[8,1,1024]{2,0,1:T(8,128)(2,1)S(1)}, bf16[8,1,1024]{2,0,1:T(8,128)(2,1)S(1)}, u32[]{:S(2)}, u32[]{:S(2)}) collective-permute-start(bf16[8,1,1024]{2,0,1:T(8,128)(2,1)S(1)} %copy.117), channel_id=1, source_target_pairs={{0,1},{1,2},{2,3},{4,5},{5,6},{6,7},{8,9},{9,10},{10,11},{12,13},{... | collective-permute-start | bytes 49160 | tf_op jit(solution)/shard_map/ppermute | solution.py:23
  42.2 1.4 copy-start
  43.6 22.2 %collective-permute-start.2 = (bf16[1,34,1024]{1,2,0:T(8,128)(2,1)S(1)}, bf16[1,34,1024]{1,2,0:T(8,128)(2,1)S(1)}, u32[]{:S(2)}, u32[]{:S(2)}) collective-permute-start(bf16[1,34,1024]{1,2,0:T(8,128)(2,1)S(1)} %slice_select_fusion), channel_id=1, source_target_pairs={{0,4},{4,0},{8,12},{12,8},{16,20},{20,16},{24,28},{28,24},{32,36},... | collective-permute-start | bytes 208904 | tf_op jit(solution)/shard_map/ppermute | solution.py:35
  45.5 3.9 %copy-start.1 = (bf16[8,34,1024]{1,2,0:T(8,128)(2,1)S(1)}, bf16[8,34,1024]{1,2,0:T(8,128)(2,1)}, u32[]{:S(2)}) copy-start(bf16[8,34,1024]{1,2,0:T(8,128)(2,1)} %copy-done) | copy-start | bytes 1671172
  90.7 10.6 %copy-start.3 = (bf16[256,128,1,8]{0,3,1,2:T(8,128)(2,1)S(1)}, bf16[256,128,1,8]{0,3,1,2:T(8,128)(2,1)}, u32[]{:S(2)}) copy-start(bf16[256,128,1,8]{0,3,1,2:T(8,128)(2,1)} %stack_reshape.30) | copy-start | bytes 1572868
  90.7 11.4 %copy-start.4 = (bf16[256,128,1,8]{0,3,1,2:T(8,128)(2,1)S(1)}, bf16[256,128,1,8]{0,3,1,2:T(8,128)(2,1)}, u32[]{:S(2)}) copy-start(bf16[256,128,1,8]{0,3,1,2:T(8,128)(2,1)} %stack_reshape.31) | copy-start | bytes 1572868
  95.5 7.5 %copy-start.5 = (bf16[256,128,1,8]{0,3,1,2:T(8,128)(2,1)S(1)}, bf16[256,128,1,8]{0,3,1,2:T(8,128)(2,1)}, u32[]{:S(2)}) copy-start(bf16[256,128,1,8]{0,3,1,2:T(8,128)(2,1)} %stack_reshape.32) | copy-start | bytes 1572868
  95.5 8.3 %copy-start.6 = (bf16[256,128,1,8]{0,3,1,2:T(8,128)(2,1)S(1)}, bf16[256,128,1,8]{0,3,1,2:T(8,128)(2,1)}, u32[]{:S(2)}) copy-start(bf16[256,128,1,8]{0,3,1,2:T(8,128)(2,1)} %stack_reshape.33) | copy-start | bytes 1572868
  95.5 9.1 %copy-start.7 = (bf16[256,128,1,8]{0,3,1,2:T(8,128)(2,1)S(1)}, bf16[256,128,1,8]{0,3,1,2:T(8,128)(2,1)}, u32[]{:S(2)}) copy-start(bf16[256,128,1,8]{0,3,1,2:T(8,128)(2,1)} %stack_reshape.34) | copy-start | bytes 1572868
  95.5 10.0 %copy-start.8 = (bf16[256,128,1,8]{0,3,1,2:T(8,128)(2,1)S(1)}, bf16[256,128,1,8]{0,3,1,2:T(8,128)(2,1)}, u32[]{:S(2)}) copy-start(bf16[256,128,1,8]{0,3,1,2:T(8,128)(2,1)} %stack_reshape.35) | copy-start | bytes 1572868
  123.2 113.8 %all-gather.11.cloned.1.call-start = ((), (), s32[]{:S(2)}) async-start(), calls=%async_computation.4 | async-start | bytes 18874368 | tf_op jit(solution)/shard_map/all_gather | solution.py:112
  237.0 23.0 %copy-start.10 = (s32[8]{0:T(128)S(1)}, s32[8]{0:T(128)}, u32[]{:S(2)}) copy-start(s32[8]{0:T(128)} %param.9) | copy-start | bytes 100
  237.0 23.1 %copy-start.9 = (s32[16]{0:T(128)S(1)}, s32[16]{0:T(128)}, u32[]{:S(2)}) copy-start(s32[16]{0:T(128)} %param.8) | copy-start | bytes 196
  246.5 29.4 %all-to-all-start = ((bf16[16,16,512]{2,1,0:T(8,128)(2,1)}), bf16[16,16,512]{2,1,0:T(8,128)(2,1)S(1)}, u32[]{:S(2)}, u32[]{:S(2)}) async-start(bf16[16,16,512]{2,1,0:T(8,128)(2,1)} %bitcast.10), calls=%async_computation | async-start | bytes 524288 | tf_op jit(solution)/shard_map/all_to_all | solution.py:120
  282.7 49.5 %copy-start.2 = (bf16[8,32,1024]{2,1,0:T(8,128)(2,1)S(1)}, bf16[8,32,1024]{2,1,0:T(8,128)(2,1)}, u32[]{:S(2)}) copy-start(bf16[8,32,1024]{2,1,0:T(8,128)(2,1)} %param.5) | copy-start | bytes 1572868
Sparse Core Ops, SparseCore 0:
  9.4 69.2 all-gather.6
  123.3 73.9 all-gather.8
  199.4 37.5 all-gather.10

commit v4 on v3

--- a/solution.py
+++ b/solution.py
@@ -99,21 +99,21 @@
             padded[1 + shift_amount : 1 + shift_amount + rows_dev] * inside[:, None, None]
         )
     tokens = rows_dev * cols_dev
-    taps = []
-    for row_tap in range(3):
-        for column_kernel_tap in range(3):
-            patches = windows[row_tap][:, column_kernel_tap : column_kernel_tap + cols_dev, :]
-            taps.append(patches.reshape(tokens, -1, block_in))
-    im2col = jnp.stack(taps, axis=2).reshape(tokens, -1, spatial_rows)
-    pad_rows = along_z.shape[1] - spatial_rows
-    im2col = jnp.pad(im2col, ((0, 0), (0, 0), (0, pad_rows)))
-    along_z, im2col = lax.optimization_barrier((along_z, im2col))
+    along_z, *windows = lax.optimization_barrier((along_z, *windows))
     whole = lax.all_gather(along_z, ("xhi", "xlo"), axis=0)
     whole = lax.all_gather(whole, "core", axis=0)
     whole = whole.reshape((-1,) + along_z.shape[1:])
-    running = lax.dot_general(
-        im2col, whole, (((1, 2), (0, 1)), ((), ())), preferred_element_type=jnp.float32
-    )
+    running = jnp.zeros((tokens, middle), jnp.float32)
+    for row_tap in range(3):
+        for column_kernel_tap in range(3):
+            tap = 3 * row_tap + column_kernel_tap
+            patches = windows[row_tap][:, column_kernel_tap : column_kernel_tap + cols_dev, :]
+            running = running + lax.dot_general(
+                patches.reshape(tokens, -1, block_in),
+                whole[:, tap * block_in : (tap + 1) * block_in, :],
+                (((1, 2), (0, 1)), ((), ())),
+                preferred_element_type=jnp.float32,
+            )
     hidden = jax.nn.gelu(running).astype(jnp.bfloat16)
     group_size = lax.axis_size(FRAME_AXES)
     per_pixel = tokens // group_size
@@ -136,11 +136,12 @@
         stacked_panels, temporal_w, (((1, 2), (2, 3)), ((), ())), preferred_element_type=jnp.float32
     )
     result = result.reshape(FRAMES * per_pixel, channels)
-    mixed_out = from_gathered_order(result.astype(jnp.bfloat16), block_out)
+    mixed_out = result.astype(jnp.bfloat16)
     returned = lax.all_to_all(
         mixed_out.reshape(group_size, per_pixel, channels), FRAME_AXES, 0, 0, tiled=True
     )
-    update = returned.reshape(rows_dev, cols_dev, channels)
+    update = from_gathered_order(returned.reshape(tokens, channels), block_out)
+    update = update.reshape(rows_dev, cols_dev, channels)
     return (values + update.astype(jnp.float32)).astype(jnp.bfloat16)
 
 

time: 341 us -> 323 us (0.947)
  local copies, waits for them, and re-layouts: 113 us -> 98.8 us
    all_gather x1, waiting for transfers between devices: 39.7 us -> 0.02 us  [shards(): whole = lax.all_gather(whole, 'core', axis=0)]
    another operation x13 -> x0, local copies, waits for them, and re-layouts: 36.4 us -> none  [the longest x11 27.9 us: shards(): im2col = jnp.stack(taps, axis=2).reshape(tokens, -1, spatial_rows)]
    all_gather x1, waiting for transfers between devices: 0.01 us -> 21.4 us  [shards(): lax.all_gather(weight_rows(w_spatial, w_temporal), ('zhi', 'zlo'), axis=0)]
    reshape x0 -> x9, local copies, waits for them, and re-layouts: none -> 20.4 us  [shards(): patches.reshape(tokens, -1, block_in)]
    convert_element_type x1 -> x5, local copies, waits for them, and re-layouts: 0.2 us -> 16.7 us  [shards(): return (values + update.astype(jnp.float32)).astype(jnp.bfloat16)]
    ppermute x1, waiting for transfers between devices: 0.01 us -> 8.34 us  [partner(): return lax.ppermute(value, axis, pairs)]
    all_gather x1, waiting for transfers between devices: 74 us -> 80.5 us  [shards(): whole = lax.all_gather(along_z, ('xhi', 'xlo'), axis=0)]
    pad x1 -> x0, local copies, waits for them, and re-layouts: 5.93 us -> none  [shards(): im2col = jnp.pad(im2col, ((0, 0), (0, 0), (0, pad_rows)))]
  transfers between devices with their start and end apart: 7 -> 7, of which waited for: 3 -> 4; matrix products, arithmetic and copies ran while one was open for 31% -> 25% of each run, Pallas kernels for 0% -> 0%
where the time goes in v4:
time: 323 us; the launch traced here: 322 us
  waiting for transfers between devices  120 us (37%)
  local copies, waits for them, and re-layouts  98.8 us (31%)
  blocking collectives  40.8 us (13%)
  starting transfers between devices  25.9 us (8%)
  between operations  13.5 us (4%)
  other arithmetic  12.4 us (4%)
  matrix products  10.9 us (3%)
    all_gather x1, waiting for transfers between devices, shards(): whole = lax.all_gather(along_z, ('xhi', 'xlo'), axis=0)  80.5 us
    all_to_all x1, blocking collectives, shards(): lax.all_to_all(mixed_out.reshape(group_size, per_pixel, channels), FRAME_...  40.8 us
    slice x12, local copies, waits for them, and re-layouts, shards(): windows[row_tap][:, column_kernel_tap:column_kernel_tap + cols_dev, :]  27.8 us
    all_gather x1, waiting for transfers between devices, shards(): lax.all_gather(weight_rows(w_spatial, w_temporal), ('zhi', 'zlo'), axis=0)  21.4 us
    reshape x9, local copies, waits for them, and re-layouts, shards(): patches.reshape(tokens, -1, block_in)  20.4 us
    convert_element_type x5, local copies, waits for them, and re-layouts, shards(): return (values + update.astype(jnp.float32)).astype(jnp.bfloat16)  16.7 us
    all_to_all x1, starting transfers between devices, shards(): lax.all_to_all(hidden.reshape(group_size, per_pixel, middle), FRAME_AXES,...  13.7 us
    all_to_all x1, waiting for transfers between devices, shards(): lax.all_to_all(hidden.reshape(group_size, per_pixel, middle), FRAME_AXES,...  9.46 us
  transfers between devices with their start and end apart: 7, of which 4 were waited for; matrix products, arithmetic and copies ran while one was open for 25% of the time, Pallas kernels for 0%

profile of v4, /device:TPU:1, one launch (start us, length us, event | category | flops | bytes accessed | tf_op | source)
XLA Modules:
  0.0 322.1 jit_solution(6662031656644255499)
XLA Ops:
  14.5 2.2 copy.119
  16.7 2.7 fusion.52
  21.4 4.5 %collective-permute-start = (bf16[8,1,1024]{2,0,1:T(8,128)(2,1)S(1)}, bf16[8,1,1024]{2,0,1:T(8,128)(2,1)S(1)}, u32[]{:S(2)}, u32[]{:S(2)}) collective-permute-start(bf16[8,1,1024]{2,0,1:T(8,128)(2,1)S(1)} %copy.120), channel_id=1, source_target_pairs={{0,1},{1,2},{2,3},{4,5},{5,6},{6,7},{8,9},{9,10},{10,11},{12,13},{... | collective-permute-start | bytes 49160 | tf_op jit(solution)/shard_map/ppermute | solution.py:23
  27.9 5.6 %collective-permute-start.1 = (bf16[8,1,1024]{2,0,1:T(8,128)(2,1)S(1)}, bf16[8,1,1024]{2,0,1:T(8,128)(2,1)S(1)}, u32[]{:S(2)}, u32[]{:S(2)}) collective-permute-start(bf16[8,1,1024]{2,0,1:T(8,128)(2,1)S(1)} %copy.121), channel_id=1, source_target_pairs={{1,0},{2,1},{3,2},{5,4},{6,5},{7,6},{9,8},{10,9},{11,10},{13,12},{... | collective-permute-start | bytes 49160 | tf_op jit(solution)/shard_map/ppermute | solution.py:25
  37.2 5.7 %broadcast_multiply_fusion = (bf16[8,34,1024]{1,2,0:T(8,128)(2,1)}, bf16[8,34,1024]{1,2,0:T(8,128)(2,1)S(1)}) fusion(bf16[8]{0:T(256)(128)(2,1)S(1)} %and_convert_fusion.1, bf16[8,1,1024]{1,2,0:T(8,128)(2,1)} %copy.123, bf16[8,32,1024]{1,2,0:T(8,128)(2,1)S(1)} %bitcast.101, bf16[8,1,1024]{1,2,0:T(8,128)(2,1)} %copy.122), kind=kLoop, calls=%fused_computation.41 | loop fusion | flops 2506752 | bytes 1671184 | tf_op jit(solution)/shard_map/mul | solution.py:99
  48.3 8.3 %collective-permute-done.2 = bf16[1,34,1024]{1,2,0:T(8,128)(2,1)S(1)} collective-permute-done((bf16[1,34,1024]{1,2,0:T(8,128)(2,1)S(1)}, bf16[1,34,1024]{1,2,0:T(8,128)(2,1)S(1)}, u32[]{:S(2)}, u32[]{:S(2)}) %collective-permute-start.2) | collective-permute-done | bytes 69664 | tf_op jit(solution)/shard_map/ppermute | solution.py:35
  57.2 21.4 %all-gather.7.cloned.1.call-done = bf16[1536,512]{1,0:T(8,128)(2,1)} async-done(((bf16[96,512]{1,0:T(8,128)(2,1)}), bf16[1536,512]{1,0:T(8,128)(2,1)}) %all-gather.7.cloned.1.call-update) | async-done | bytes 1572880 | tf_op jit(solution)/shard_map/all_gather | solution.py:77
  78.8 80.5 %all-gather.9.cloned.1.call-done = bf16[64,96,512]{2,1,0:T(8,128)(2,1)} async-done(((bf16[16,96,512]{2,1,0:T(8,128)(2,1)}), bf16[64,96,512]{2,1,0:T(8,128)(2,1)}) %all-gather.9.cloned.1.call-update) | async-done | bytes 6291472 | tf_op jit(solution)/shard_map/all_gather | solution.py:103
  160.7 2.5 copy.129
  163.2 2.2 reshape.149
  165.4 2.5 copy.130
  170.1 2.5 copy.128
  172.6 3.8 %reshape.147 = bf16[256,128,8]{0,2,1:T(8,128)(2,1)} reshape(bf16[8,32,1024]{1,0,2:T(8,128)(2,1)} %copy.128) | data formatting | bytes 1048576 | tf_op jit(solution)/shard_map/reshape | solution.py:112
  176.4 3.6 %fusion.51 = (bf16[8,32,1024]{1,2,0:T(8,128)(2,1)}, bf16[8,32,1024]{1,2,0:T(8,128)(2,1)S(1)}, bf16[8,32,1024]{1,2,0:T(8,128)(2,1)}) fusion(bf16[8,34,1024]{1,2,0:T(8,128)(2,1)S(1)} %copy-done), kind=kLoop, calls=%fused_computation.76 | loop fusion | bytes 3145728 | tf_op jit(solution)/shard_map/slice | solution.py:110
  181.4 2.2 reshape.152
  183.5 3.4 %copy.131 = bf16[8,32,1024]{1,0,2:T(8,128)(2,1)S(1)} copy(bf16[8,32,1024]{1,2,0:T(8,128)(2,1)} %get-tuple-element.17) | data formatting | bytes 1048576 | tf_op jit(solution)/shard_map/slice | solution.py:110
  186.9 2.2 reshape.151
  189.1 3.6 %copy.133 = bf16[8,32,1024]{1,0,2:T(8,128)(2,1)S(1)} copy(bf16[8,32,1024]{1,2,0:T(8,128)(2,1)} %get-tuple-element.15) | data formatting | bytes 1048576 | tf_op jit(solution)/shard_map/slice | solution.py:110
  192.7 2.2 reshape.153
  196.1 2.6 copy.134
  198.7 2.2 reshape.154
  202.5 2.2 reshape.156
  209.7 3.0 copy-done.4
  220.9 13.7 %all-to-all-start = ((bf16[16,16,512]{2,1,0:T(8,128)(2,1)}), bf16[16,16,512]{2,1,0:T(8,128)(2,1)S(1)}, u32[]{:S(2)}, u32[]{:S(2)}) async-start(bf16[16,16,512]{2,1,0:T(8,128)(2,1)} %bitcast.17), calls=%async_computation | async-start | bytes 524288 | tf_op jit(solution)/shard_map/all_to_all | solution.py:120
  236.9 4.3 %dot_general.45 = bf16[1024,3,512]{2,1,0:T(4,128)(2,1)} reshape(bf16[128,24,512]{2,1,0:T(8,128)(2,1)S(1)} %slice.115) | data formatting | bytes 6291456 | tf_op jit(solution)/shard_map/dot_general | solution.py:135
  241.2 9.5 %all-to-all-done = bf16[16,16,512]{2,1,0:T(8,128)(2,1)S(1)} async-done(((bf16[16,16,512]{2,1,0:T(8,128)(2,1)}), bf16[16,16,512]{2,1,0:T(8,128)(2,1)S(1)}, u32[]{:S(2)}, u32[]{:S(2)}) %all-to-all-start) | async-done | bytes 262176 | tf_op jit(solution)/shard_map/all_to_all | solution.py:120
  253.8 3.4 %fusion.6 = bf16[256,1024]{1,0:T(8,128)(2,1)S(1)} fusion(bf16[256,3,512]{2,0,1:T(8,128)(2,1)S(1)} %reshape.159, bf16[1024,3,512]{2,1,0:T(4,128)(2,1)} %dot_general.45), kind=kOutput, calls=%fused_computation.9 | convolution fusion | flops 805568512 | bytes 4456448 | tf_op jit(solution)/shard_map/dot_general | solution.py:135
  257.1 40.8 %all_to_all.10 = bf16[16,16,1024]{2,1,0:T(8,128)(2,1)S(1)} all-to-all(bf16[16,16,1024]{2,1,0:T(8,128)(2,1)S(1)} %bitcast.117), channel_id=1, replica_groups=mesh['clip'=4,'xhi'=2,'zhi'=8,'zlo'=2,'xlo'=2,'core'=2] {'xhi','zhi'}, dimensions={0} | all-to-all | bytes 1048576 | tf_op jit(solution)/shard_map/all_to_all | solution.py:140
  297.9 5.2 %copy.140 = f32[16,16,1024]{1,0,2:T(8,128)} copy(bf16[16,16,1024]{2,1,0:T(8,128)(2,1)S(1)} %all_to_all.10) | data formatting | bytes 1572864 | tf_op jit(solution)/shard_map/convert_element_type | solution.py:145
  303.1 6.1 %reshape.162 = f32[256,2,2,2,16,8]{0,5,4,3,2,1:T(8,128)S(1)} reshape(f32[16,16,1024]{1,0,2:T(8,128)} %copy.140) | data formatting | bytes 2097152 | tf_op jit(solution)/shard_map/convert_element_type | solution.py:145
  309.3 2.5 reshape.161
  311.8 2.9 copy.142
  (86 shorter events, 49.0 us)
Async XLA Ops:
  6.5 72.1 %all-gather.7.cloned.1.call-start = ((), (), s32[]{:S(2)}) async-start(), calls=%async_computation.2 | async-start | bytes 1671168 | tf_op jit(solution)/shard_map/all_gather | solution.py:77
  8.9 150.5 %all-gather.9.cloned.1.call-start = ((), (), s32[]{:S(2)}) async-start(), calls=%async_computation.3 | async-start | bytes 7864320 | tf_op jit(solution)/shard_map/all_gather | solution.py:103
  21.4 12.1 %collective-permute-start = (bf16[8,1,1024]{2,0,1:T(8,128)(2,1)S(1)}, bf16[8,1,1024]{2,0,1:T(8,128)(2,1)S(1)}, u32[]{:S(2)}, u32[]{:S(2)}) collective-permute-start(bf16[8,1,1024]{2,0,1:T(8,128)(2,1)S(1)} %copy.120), channel_id=1, source_target_pairs={{0,1},{1,2},{2,3},{4,5},{5,6},{6,7},{8,9},{9,10},{10,11},{12,13},{... | collective-permute-start | bytes 49160 | tf_op jit(solution)/shard_map/ppermute | solution.py:23
  27.9 7.5 %collective-permute-start.1 = (bf16[8,1,1024]{2,0,1:T(8,128)(2,1)S(1)}, bf16[8,1,1024]{2,0,1:T(8,128)(2,1)S(1)}, u32[]{:S(2)}, u32[]{:S(2)}) collective-permute-start(bf16[8,1,1024]{2,0,1:T(8,128)(2,1)S(1)} %copy.121), channel_id=1, source_target_pairs={{1,0},{2,1},{3,2},{5,4},{6,5},{7,6},{9,8},{10,9},{11,10},{13,12},{... | collective-permute-start | bytes 49160 | tf_op jit(solution)/shard_map/ppermute | solution.py:25
  42.9 1.3 copy-start.1
  44.3 12.3 %collective-permute-start.2 = (bf16[1,34,1024]{1,2,0:T(8,128)(2,1)S(1)}, bf16[1,34,1024]{1,2,0:T(8,128)(2,1)S(1)}, u32[]{:S(2)}, u32[]{:S(2)}) collective-permute-start(bf16[1,34,1024]{1,2,0:T(8,128)(2,1)S(1)} %slice_select_fusion), channel_id=1, source_target_pairs={{0,4},{4,0},{8,12},{12,8},{16,20},{20,16},{24,28},{28,24},{32,36},... | collective-permute-start | bytes 208904 | tf_op jit(solution)/shard_map/ppermute | solution.py:35
  78.6 129.2 %all-gather.11.cloned.1.call-start = ((), (), s32[]{:S(2)}) async-start(), calls=%async_computation.4 | async-start | bytes 18874368 | tf_op jit(solution)/shard_map/all_gather | solution.py:104
  170.1 6.3 %copy-start = (bf16[8,34,1024]{1,2,0:T(8,128)(2,1)S(1)}, bf16[8,34,1024]{1,2,0:T(8,128)(2,1)}, u32[]{:S(2)}) copy-start(bf16[8,34,1024]{1,2,0:T(8,128)(2,1)} %get-tuple-element.11) | copy-start | bytes 1671172
  196.1 4.8 %copy-start.3 = (bf16[8,32,1024]{2,1,0:T(8,128)(2,1)S(1)}, bf16[8,32,1024]{2,1,0:T(8,128)(2,1)}, u32[]{:S(2)}) copy-start(bf16[8,32,1024]{2,1,0:T(8,128)(2,1)} %get-tuple-element.21) | copy-start | bytes 1572868
  204.6 3.1 copy-start.6
  207.8 4.9 %copy-start.4 = (bf16[8,16,96,512]{3,2,1,0:T(8,128)(2,1)S(1)}, bf16[8,16,96,512]{3,2,1,0:T(8,128)(2,1)}, u32[]{:S(2)}) copy-start(bf16[8,16,96,512]{3,2,1,0:T(8,128)(2,1)} %all-gather.11.cloned.1.call-done) | copy-start | bytes 37748740
  207.8 4.9 %copy-start.7 = (bf16[256,128,8]{0,2,1:T(8,128)(2,1)S(1)}, bf16[256,128,8]{0,2,1:T(8,128)(2,1)}, u32[]{:S(2)}) copy-start(bf16[256,128,8]{0,2,1:T(8,128)(2,1)} %reshape.150) | copy-start | bytes 1572868
  212.7 1.0 copy-start.10
  213.8 1.0 copy-start.11
  214.8 1.0 copy-start.12
  215.9 1.0 copy-start.5
  216.9 1.0 copy-start.8
  217.9 1.0 copy-start.9
  219.5 15.1 %copy-start.14 = (s32[8]{0:T(128)S(1)}, s32[8]{0:T(128)}, u32[]{:S(2)}) copy-start(s32[8]{0:T(128)} %param.9) | copy-start | bytes 100
  219.5 15.1 %copy-start.13 = (s32[16]{0:T(128)S(1)}, s32[16]{0:T(128)}, u32[]{:S(2)}) copy-start(s32[16]{0:T(128)} %param.8) | copy-start | bytes 196
  220.9 29.8 %all-to-all-start = ((bf16[16,16,512]{2,1,0:T(8,128)(2,1)}), bf16[16,16,512]{2,1,0:T(8,128)(2,1)S(1)}, u32[]{:S(2)}, u32[]{:S(2)}) async-start(bf16[16,16,512]{2,1,0:T(8,128)(2,1)} %bitcast.17), calls=%async_computation | async-start | bytes 524288 | tf_op jit(solution)/shard_map/all_to_all | solution.py:120
  311.8 2.9 copy-start.2
Sparse Core Ops, SparseCore 0:
  9.4 69.1 all-gather.6
  80.7 78.6 all-gather.8
  161.5 37.5 all-gather.10

commit v5 on v3

--- a/solution.py
+++ b/solution.py
@@ -99,21 +99,25 @@
             padded[1 + shift_amount : 1 + shift_amount + rows_dev] * inside[:, None, None]
         )
     tokens = rows_dev * cols_dev
-    taps = []
+    patches = []
     for row_tap in range(3):
         for column_kernel_tap in range(3):
-            patches = windows[row_tap][:, column_kernel_tap : column_kernel_tap + cols_dev, :]
-            taps.append(patches.reshape(tokens, -1, block_in))
-    im2col = jnp.stack(taps, axis=2).reshape(tokens, -1, spatial_rows)
-    pad_rows = along_z.shape[1] - spatial_rows
-    im2col = jnp.pad(im2col, ((0, 0), (0, 0), (0, pad_rows)))
-    along_z, im2col = lax.optimization_barrier((along_z, im2col))
+            window = windows[row_tap][:, column_kernel_tap : column_kernel_tap + cols_dev, :]
+            patches.append(window.reshape(tokens, -1, block_in))
+    early = 3
+    along_z, *head = lax.optimization_barrier((along_z, *patches[:early]))
+    patches[:early] = head
     whole = lax.all_gather(along_z, ("xhi", "xlo"), axis=0)
     whole = lax.all_gather(whole, "core", axis=0)
     whole = whole.reshape((-1,) + along_z.shape[1:])
-    running = lax.dot_general(
-        im2col, whole, (((1, 2), (0, 1)), ((), ())), preferred_element_type=jnp.float32
-    )
+    running = jnp.zeros((tokens, middle), jnp.float32)
+    for tap, patch in enumerate(patches):
+        running = running + lax.dot_general(
+            patch,
+            whole[:, tap * block_in : (tap + 1) * block_in, :],
+            (((1, 2), (0, 1)), ((), ())),
+            preferred_element_type=jnp.float32,
+        )
     hidden = jax.nn.gelu(running).astype(jnp.bfloat16)
     group_size = lax.axis_size(FRAME_AXES)
     per_pixel = tokens // group_size
@@ -131,12 +135,13 @@
         "gkfe,epgc->fpkgc", selector_matrix, frame_sequence, preferred_element_type=jnp.float32
     )
     stacked_panels = stacked_panels.astype(jnp.bfloat16).reshape(FRAMES * per_pixel, 3, middle)
-    temporal_w = whole[:, spatial_rows:, :].reshape(whole.shape[0], block_out, 3, middle)
+    xhi, z, xlo, core = channel_dims()
+    temporal_w = whole[:, spatial_rows:, :].reshape(core, xhi, xlo, z, block_out, 3, middle)
+    temporal_w = temporal_w.transpose(1, 3, 2, 0, 4, 5, 6).reshape(channels, 3, middle)
     result = lax.dot_general(
-        stacked_panels, temporal_w, (((1, 2), (2, 3)), ((), ())), preferred_element_type=jnp.float32
+        stacked_panels, temporal_w, (((1, 2), (1, 2)), ((), ())), preferred_element_type=jnp.float32
     )
-    result = result.reshape(FRAMES * per_pixel, channels)
-    mixed_out = from_gathered_order(result.astype(jnp.bfloat16), block_out)
+    mixed_out = result.astype(jnp.bfloat16)
     returned = lax.all_to_all(
         mixed_out.reshape(group_size, per_pixel, channels), FRAME_AXES, 0, 0, tiled=True
     )

time: 341 us -> 297 us (0.87)
  local copies, waits for them, and re-layouts: 113 us -> 80.3 us
  waiting for transfers between devices: 121 us -> 113 us
    another operation x13 -> x0, local copies, waits for them, and re-layouts: 36.4 us -> none  [the longest x11 27.9 us: shards(): im2col = jnp.stack(taps, axis=2).reshape(tokens, -1, spatial_rows)]
    all_gather x1, waiting for transfers between devices: 39.7 us -> 7.9 us  [shards(): whole = lax.all_gather(whole, 'core', axis=0)]
    reshape x0 -> x9, local copies, waits for them, and re-layouts: none -> 19 us  [shards(): patches.append(window.reshape(tokens, -1, block_in))]
    ppermute x1, waiting for transfers between devices: 0.01 us -> 8.35 us  [partner(): return lax.ppermute(value, axis, pairs)]
    all_gather x1, waiting for transfers between devices: 0.01 us -> 7 us  [shards(): lax.all_gather(weight_rows(w_spatial, w_temporal), ('zhi', 'zlo'), axis=0)]
    all_gather x1, waiting for transfers between devices: 74 us -> 80.5 us  [shards(): whole = lax.all_gather(along_z, ('xhi', 'xlo'), axis=0)]
    pad x1 -> x0, local copies, waits for them, and re-layouts: 5.93 us -> none  [shards(): im2col = jnp.pad(im2col, ((0, 0), (0, 0), (0, pad_rows)))]
    dot_general x1 -> x0, local copies, waits for them, and re-layouts: 4.3 us -> none  [shards(): lax.dot_general(stacked_panels, temporal_w, (((1, 2), (2, 3)), ((), ())),...]
  transfers between devices with their start and end apart: 7 -> 7, of which waited for: 3 -> 5; matrix products, arithmetic and copies ran while one was open for 31% -> 26% of each run, Pallas kernels for 0% -> 0%
where the time goes in v5:
time: 297 us; the launch traced here: 296 us
  waiting for transfers between devices  113 us (38%)
  local copies, waits for them, and re-layouts  80.3 us (27%)
  blocking collectives  40.9 us (14%)
  starting transfers between devices  25.7 us (9%)
  between operations  13.5 us (5%)
  other arithmetic  12.5 us (4%)
  matrix products  10.5 us (4%)
    all_gather x1, waiting for transfers between devices, shards(): whole = lax.all_gather(along_z, ('xhi', 'xlo'), axis=0)  80.5 us
    all_to_all x1, blocking collectives, shards(): lax.all_to_all(mixed_out.reshape(group_size, per_pixel, channels), FRAME_...  40.9 us
    slice x12, local copies, waits for them, and re-layouts, shards(): windows[row_tap][:, column_kernel_tap:column_kernel_tap + cols_dev, :]  25.6 us
    reshape x9, local copies, waits for them, and re-layouts, shards(): patches.append(window.reshape(tokens, -1, block_in))  19 us
    all_to_all x1, starting transfers between devices, shards(): lax.all_to_all(hidden.reshape(group_size, per_pixel, middle), FRAME_AXES,...  13.4 us
    unnamed x30, local copies, waits for them, and re-layouts  9.27 us
    all_to_all x1, waiting for transfers between devices, shards(): lax.all_to_all(hidden.reshape(group_size, per_pixel, middle), FRAME_AXES,...  9.11 us
    ppermute x1, waiting for transfers between devices, partner(): return lax.ppermute(value, axis, pairs)  8.35 us
  transfers between devices with their start and end apart: 7, of which 5 were waited for; matrix products, arithmetic and copies ran while one was open for 26% of the time, Pallas kernels for 0%

profile of v5, /device:TPU:1, one launch (start us, length us, event | category | flops | bytes accessed | tf_op | source)
XLA Modules:
  0.0 296.2 jit_solution(17890725404274386129)
XLA Ops:
  14.5 2.2 copy.122
  16.7 2.7 fusion.45
  21.4 4.5 %collective-permute-start = (bf16[8,1,1024]{2,0,1:T(8,128)(2,1)S(1)}, bf16[8,1,1024]{2,0,1:T(8,128)(2,1)S(1)}, u32[]{:S(2)}, u32[]{:S(2)}) collective-permute-start(bf16[8,1,1024]{2,0,1:T(8,128)(2,1)S(1)} %copy.123), channel_id=1, source_target_pairs={{0,1},{1,2},{2,3},{4,5},{5,6},{6,7},{8,9},{9,10},{10,11},{12,13},{... | collective-permute-start | bytes 49160 | tf_op jit(solution)/shard_map/ppermute | solution.py:23
  25.9 2.0 copy.124
  27.9 5.6 %collective-permute-start.1 = (bf16[8,1,1024]{2,0,1:T(8,128)(2,1)S(1)}, bf16[8,1,1024]{2,0,1:T(8,128)(2,1)S(1)}, u32[]{:S(2)}, u32[]{:S(2)}) collective-permute-start(bf16[8,1,1024]{2,0,1:T(8,128)(2,1)S(1)} %copy.124), channel_id=1, source_target_pairs={{1,0},{2,1},{3,2},{5,4},{6,5},{7,6},{9,8},{10,9},{11,10},{13,12},{... | collective-permute-start | bytes 49160 | tf_op jit(solution)/shard_map/ppermute | solution.py:25
  37.2 5.7 %broadcast_multiply_fusion = (bf16[8,34,1024]{1,2,0:T(8,128)(2,1)}, bf16[8,34,1024]{1,2,0:T(8,128)(2,1)S(1)}) fusion(bf16[8]{0:T(256)(128)(2,1)S(1)} %and_convert_fusion.1, bf16[8,1,1024]{1,2,0:T(8,128)(2,1)} %copy.126, bf16[8,32,1024]{1,2,0:T(8,128)(2,1)S(1)} %bitcast.103, bf16[8,1,1024]{1,2,0:T(8,128)(2,1)} %copy.125), kind=kLoop, calls=%fused_computation.39 | loop fusion | flops 2506752 | bytes 1671184 | tf_op jit(solution)/shard_map/mul | solution.py:99
  46.3 2.0 copy.128
  48.3 8.3 %collective-permute-done.2 = bf16[1,34,1024]{1,2,0:T(8,128)(2,1)S(1)} collective-permute-done((bf16[1,34,1024]{1,2,0:T(8,128)(2,1)S(1)}, bf16[1,34,1024]{1,2,0:T(8,128)(2,1)S(1)}, u32[]{:S(2)}, u32[]{:S(2)}) %collective-permute-start.2) | collective-permute-done | bytes 69664 | tf_op jit(solution)/shard_map/ppermute | solution.py:35
  58.5 2.5 copy.129
  61.0 2.2 reshape.148
  63.2 2.5 copy.130
  65.7 2.2 reshape.149
  69.5 2.1 reshape.150
  71.7 7.0 %all-gather.7.cloned.1.call-done = bf16[1536,512]{1,0:T(8,128)(2,1)} async-done(((bf16[96,512]{1,0:T(8,128)(2,1)}), bf16[1536,512]{1,0:T(8,128)(2,1)}) %all-gather.7.cloned.1.call-update) | async-done | bytes 1572880 | tf_op jit(solution)/shard_map/all_gather | solution.py:77
  78.9 80.5 %all-gather.9.cloned.1.call-done = bf16[64,96,512]{2,1,0:T(8,128)(2,1)} async-done(((bf16[16,96,512]{2,1,0:T(8,128)(2,1)}), bf16[64,96,512]{2,1,0:T(8,128)(2,1)}) %all-gather.9.cloned.1.call-update) | async-done | bytes 6291472 | tf_op jit(solution)/shard_map/all_gather | solution.py:110
  161.0 3.3 %fusion.44 = (bf16[8,32,1024]{1,2,0:T(8,128)(2,1)}, bf16[8,32,1024]{1,2,0:T(8,128)(2,1)S(1)}, bf16[8,32,1024]{1,2,0:T(8,128)(2,1)}) fusion(bf16[8,34,1024]{1,2,0:T(8,128)(2,1)S(1)} %copy-done), kind=kLoop, calls=%fused_computation.74 | loop fusion | bytes 3145728 | tf_op jit(solution)/shard_map/slice | solution.py:105
  165.6 2.2 reshape.153
  167.8 2.9 copy.132
  170.7 2.2 reshape.152
  172.9 2.9 copy.134
  175.9 2.2 reshape.154
  179.3 2.6 copy.137
  181.9 2.2 reshape.155
  185.7 2.2 reshape.157
  191.2 7.9 %all-gather.11.cloned.1.call-done = bf16[8,16,96,512]{3,2,1,0:T(8,128)(2,1)} async-done(((bf16[4,16,96,512]{3,2,1,0:T(8,128)(2,1)}), bf16[8,16,96,512]{3,2,1,0:T(8,128)(2,1)}) %all-gather.11.cloned.1.call-update) | async-done | bytes 12582928 | tf_op jit(solution)/shard_map/all_gather | solution.py:111
  201.0 3.0 %copy-done.4 = bf16[8,16,96,512]{3,2,1,0:T(8,128)(2,1)S(1)} copy-done((bf16[8,16,96,512]{3,2,1,0:T(8,128)(2,1)S(1)}, bf16[8,16,96,512]{3,2,1,0:T(8,128)(2,1)}, u32[]{:S(2)}) %copy-start.4) | copy-done | bytes 12582936
  212.2 13.4 %all-to-all-start = ((bf16[16,16,512]{2,1,0:T(8,128)(2,1)}), bf16[16,16,512]{2,1,0:T(8,128)(2,1)S(1)}, u32[]{:S(2)}, u32[]{:S(2)}) async-start(bf16[16,16,512]{2,1,0:T(8,128)(2,1)} %bitcast.17), calls=%async_computation | async-start | bytes 524288 | tf_op jit(solution)/shard_map/all_to_all | solution.py:124
  225.8 2.1 slice.124
  229.0 3.6 %copy.143 = bf16[2,16,2,2,8,3,512]{6,4,3,2,1,0,5:T(8,128)(2,1)} copy(bf16[2,16,2,2,8,3,512]{6,1,2,0,3,5,4:T(8,128)(2,1)S(1)} %bitcast.104) | data formatting | bytes 6291456 | tf_op jit(solution)/shard_map/transpose | solution.py:140
  232.5 9.1 %all-to-all-done = bf16[16,16,512]{2,1,0:T(8,128)(2,1)S(1)} async-done(((bf16[16,16,512]{2,1,0:T(8,128)(2,1)}), bf16[16,16,512]{2,1,0:T(8,128)(2,1)S(1)}, u32[]{:S(2)}, u32[]{:S(2)}) %all-to-all-start) | async-done | bytes 262176 | tf_op jit(solution)/shard_map/all_to_all | solution.py:124
  244.8 3.0 fusion.1
  247.8 40.9 %all_to_all.10 = bf16[16,16,1024]{2,1,0:T(8,128)(2,1)S(1)} all-to-all(bf16[16,16,1024]{2,1,0:T(8,128)(2,1)S(1)} %bitcast.121), channel_id=1, replica_groups=mesh['clip'=4,'xhi'=2,'zhi'=8,'zlo'=2,'xlo'=2,'core'=2] {'xhi','zhi'}, dimensions={0} | all-to-all | bytes 1048576 | tf_op jit(solution)/shard_map/all_to_all | solution.py:145
  (82 shorter events, 45.0 us)
Async XLA Ops:
  6.5 72.1 %all-gather.7.cloned.1.call-start = ((), (), s32[]{:S(2)}) async-start(), calls=%async_computation.2 | async-start | bytes 1671168 | tf_op jit(solution)/shard_map/all_gather | solution.py:77
  8.9 150.5 %all-gather.9.cloned.1.call-start = ((), (), s32[]{:S(2)}) async-start(), calls=%async_computation.3 | async-start | bytes 7864320 | tf_op jit(solution)/shard_map/all_gather | solution.py:110
  21.4 12.1 %collective-permute-start = (bf16[8,1,1024]{2,0,1:T(8,128)(2,1)S(1)}, bf16[8,1,1024]{2,0,1:T(8,128)(2,1)S(1)}, u32[]{:S(2)}, u32[]{:S(2)}) collective-permute-start(bf16[8,1,1024]{2,0,1:T(8,128)(2,1)S(1)} %copy.123), channel_id=1, source_target_pairs={{0,1},{1,2},{2,3},{4,5},{5,6},{6,7},{8,9},{9,10},{10,11},{12,13},{... | collective-permute-start | bytes 49160 | tf_op jit(solution)/shard_map/ppermute | solution.py:23
  27.9 7.5 %collective-permute-start.1 = (bf16[8,1,1024]{2,0,1:T(8,128)(2,1)S(1)}, bf16[8,1,1024]{2,0,1:T(8,128)(2,1)S(1)}, u32[]{:S(2)}, u32[]{:S(2)}) collective-permute-start(bf16[8,1,1024]{2,0,1:T(8,128)(2,1)S(1)} %copy.124), channel_id=1, source_target_pairs={{1,0},{2,1},{3,2},{5,4},{6,5},{7,6},{9,8},{10,9},{11,10},{13,12},{... | collective-permute-start | bytes 49160 | tf_op jit(solution)/shard_map/ppermute | solution.py:25
  42.9 1.3 copy-start.1
  44.3 12.3 %collective-permute-start.2 = (bf16[1,34,1024]{1,2,0:T(8,128)(2,1)S(1)}, bf16[1,34,1024]{1,2,0:T(8,128)(2,1)S(1)}, u32[]{:S(2)}, u32[]{:S(2)}) collective-permute-start(bf16[1,34,1024]{1,2,0:T(8,128)(2,1)S(1)} %slice_select_fusion), channel_id=1, source_target_pairs={{0,4},{4,0},{8,12},{12,8},{16,20},{20,16},{24,28},{28,24},{32,36},... | collective-permute-start | bytes 208904 | tf_op jit(solution)/shard_map/ppermute | solution.py:35
  78.7 120.4 %all-gather.11.cloned.1.call-start = ((), (), s32[]{:S(2)}) async-start(), calls=%async_computation.4 | async-start | bytes 18874368 | tf_op jit(solution)/shard_map/all_gather | solution.py:111
  159.4 1.6 copy-start
  179.3 4.8 %copy-start.3 = (bf16[8,32,1024]{2,1,0:T(8,128)(2,1)S(1)}, bf16[8,32,1024]{2,1,0:T(8,128)(2,1)}, u32[]{:S(2)}) copy-start(bf16[8,32,1024]{2,1,0:T(8,128)(2,1)} %get-tuple-element.21) | copy-start | bytes 1572868
  187.9 11.2 %copy-start.6 = (bf16[256,128,8]{0,2,1:T(8,128)(2,1)S(1)}, bf16[256,128,8]{0,2,1:T(8,128)(2,1)}, u32[]{:S(2)}) copy-start(bf16[256,128,8]{0,2,1:T(8,128)(2,1)} %reshape.149) | copy-start | bytes 1572868
  199.1 4.9 %copy-start.4 = (bf16[8,16,96,512]{3,2,1,0:T(8,128)(2,1)S(1)}, bf16[8,16,96,512]{3,2,1,0:T(8,128)(2,1)}, u32[]{:S(2)}) copy-start(bf16[8,16,96,512]{3,2,1,0:T(8,128)(2,1)} %all-gather.11.cloned.1.call-done) | copy-start | bytes 37748740
  199.1 4.9 %copy-start.7 = (bf16[256,128,8]{0,2,1:T(8,128)(2,1)S(1)}, bf16[256,128,8]{0,2,1:T(8,128)(2,1)}, u32[]{:S(2)}) copy-start(bf16[256,128,8]{0,2,1:T(8,128)(2,1)} %reshape.150) | copy-start | bytes 1572868
  204.1 1.0 copy-start.10
  205.1 1.0 copy-start.11
  206.2 1.0 copy-start.12
  207.2 1.0 copy-start.5
  208.2 1.0 copy-start.8
  209.3 1.0 copy-start.9
  210.8 14.8 %copy-start.14 = (s32[8]{0:T(128)S(1)}, s32[8]{0:T(128)}, u32[]{:S(2)}) copy-start(s32[8]{0:T(128)} %param.9) | copy-start | bytes 100
  210.9 14.9 %copy-start.13 = (s32[16]{0:T(128)S(1)}, s32[16]{0:T(128)}, u32[]{:S(2)}) copy-start(s32[16]{0:T(128)} %param.8) | copy-start | bytes 196
  212.2 29.5 %all-to-all-start = ((bf16[16,16,512]{2,1,0:T(8,128)(2,1)}), bf16[16,16,512]{2,1,0:T(8,128)(2,1)S(1)}, u32[]{:S(2)}, u32[]{:S(2)}) async-start(bf16[16,16,512]{2,1,0:T(8,128)(2,1)} %bitcast.17), calls=%async_computation | async-start | bytes 524288 | tf_op jit(solution)/shard_map/all_to_all | solution.py:124
  244.8 43.9 %copy-start.2 = (bf16[8,32,1024]{2,1,0:T(8,128)(2,1)S(1)}, bf16[8,32,1024]{2,1,0:T(8,128)(2,1)}, u32[]{:S(2)}) copy-start(bf16[8,32,1024]{2,1,0:T(8,128)(2,1)} %param.5) | copy-start | bytes 1572868
Sparse Core Ops, SparseCore 0:
  9.4 69.1 all-gather.6
  80.8 78.5 all-gather.8
  161.5 37.5 all-gather.10

commit v6 on v5

--- a/solution.py
+++ b/solution.py
@@ -40,6 +40,23 @@
     return jnp.concatenate(
         [w_spatial.reshape(-1, middle), w_temporal.transpose(2, 0, 1).reshape(-1, middle)], axis=0
     )
+
+
+def ring_gather(block, axis):
+    count = lax.axis_size(axis)
+    assert count == 4
+    up = [(i, (i + 1) % count) for i in range(count)]
+    down = [(i, (i - 1) % count) for i in range(count)]
+    from_below = lax.ppermute(block, axis, up)
+    from_above = lax.ppermute(block, axis, down)
+    half = block.shape[1] // 2
+    far_low = lax.ppermute(from_below[:, :half], axis, up)
+    far_high = lax.ppermute(from_above[:, half:], axis, down)
+    far = jnp.concatenate([far_low, far_high], axis=1)
+    by_offset = jnp.stack([block, from_above, far, from_below])
+    me = lax.axis_index(axis)
+    doubled = jnp.concatenate([by_offset, by_offset])
+    return lax.dynamic_slice_in_dim(doubled, count - me, count, axis=0)
 
 
 def channel_dims():
@@ -107,14 +124,19 @@
     early = 3
     along_z, *head = lax.optimization_barrier((along_z, *patches[:early]))
     patches[:early] = head
-    whole = lax.all_gather(along_z, ("xhi", "xlo"), axis=0)
-    whole = lax.all_gather(whole, "core", axis=0)
-    whole = whole.reshape((-1,) + along_z.shape[1:])
+    split = along_z.shape[1] // 2
+    first = lax.all_gather(along_z[:, :split], ("xhi", "xlo"), axis=0)
+    second = ring_gather(along_z[:, split:], ("xhi", "xlo"))
+    halves = []
+    for part in (first, second):
+        part = lax.all_gather(part, "core", axis=0)
+        halves.append(part.reshape((-1,) + part.shape[3:]))
     running = jnp.zeros((tokens, middle), jnp.float32)
     for tap, patch in enumerate(patches):
+        row = tap * block_in
         running = running + lax.dot_general(
             patch,
-            whole[:, tap * block_in : (tap + 1) * block_in, :],
+            halves[row // split][:, row % split : row % split + block_in, :],
             (((1, 2), (0, 1)), ((), ())),
             preferred_element_type=jnp.float32,
         )
@@ -136,7 +158,7 @@
     )
     stacked_panels = stacked_panels.astype(jnp.bfloat16).reshape(FRAMES * per_pixel, 3, middle)
     xhi, z, xlo, core = channel_dims()
-    temporal_w = whole[:, spatial_rows:, :].reshape(core, xhi, xlo, z, block_out, 3, middle)
+    temporal_w = halves[1][:, spatial_rows - split :, :].reshape(core, xhi, xlo, z, block_out, 3, middle)
     temporal_w = temporal_w.transpose(1, 3, 2, 0, 4, 5, 6).reshape(channels, 3, middle)
     result = lax.dot_general(
         stacked_panels, temporal_w, (((1, 2), (1, 2)), ((), ())), preferred_element_type=jnp.float32

time: 297 us -> 296 us (level)
  waiting for transfers between devices: 113 us -> 82.5 us
  starting transfers between devices: 25.7 us -> 39.6 us
  local copies, waits for them, and re-layouts: 80.3 us -> 89.8 us
  matrix products: 10.5 us -> 14.3 us
    all_gather x2 -> x3, waiting for transfers between devices: 88.4 us -> 41 us  [the longest x2 21.4 us: shards(): part = lax.all_gather(part, 'core', axis=0)]
    ppermute x0 -> x4, waiting for transfers between devices: none -> 23.4 us  [the longest x1 8.98 us: ring_gather(): far_low = lax.ppermute(from_below[:, :half], axis, up)]
    ppermute x0 -> x4, starting transfers between devices: none -> 13.5 us  [the longest x1 5.02 us: ring_gather(): far_high = lax.ppermute(from_above[:, half:], axis, down)]
    all_gather x1, waiting for transfers between devices: 7 us -> 1.17 us  [shards(): lax.all_gather(weight_rows(w_spatial, w_temporal), ('zhi', 'zlo'), axis=0)]
    reshape x9, local copies, waits for them, and re-layouts: 19 us -> 23.9 us  [shards(): patches.append(window.reshape(tokens, -1, block_in))]
    dot_general x9, matrix products: 6.65 us -> 10.5 us  [shards(): lax.dot_general(patch, halves[row // split][:, row % split:row % split +...]
    slice x2 -> x5, local copies, waits for them, and re-layouts: 3.16 us -> 6.91 us  [the longest x2 3.16 us: shards(): halves[1][:, spatial_rows - split:, :]]
    ppermute x1, starting transfers between devices: 5.57 us -> 8.79 us  [padded_2(): lax.ppermute(head, axis, [((i + 1) % count, i) for i in range(ends)])]
  transfers between devices with their start and end apart: 7 -> 12, of which waited for: 5 -> 8; matrix products, arithmetic and copies ran while one was open for 26% -> 32% of each run, Pallas kernels for 0% -> 0%
where the time goes in v6:
time: 296 us; the launch traced here: 295 us
  local copies, waits for them, and re-layouts  89.8 us (30%)
  waiting for transfers between devices  82.5 us (28%)
  blocking collectives  40.9 us (14%)
  starting transfers between devices  39.6 us (13%)
  matrix products  14.3 us (5%)
  other arithmetic  13.8 us (5%)
  between operations  13.7 us (5%)
    all_to_all x1, blocking collectives, shards(): lax.all_to_all(mixed_out.reshape(group_size, per_pixel, channels), FRAME_...  40.9 us
    slice x12, local copies, waits for them, and re-layouts, shards(): windows[row_tap][:, column_kernel_tap:column_kernel_tap + cols_dev, :]  28.4 us
    reshape x9, local copies, waits for them, and re-layouts, shards(): patches.append(window.reshape(tokens, -1, block_in))  23.9 us
    all_gather x2, waiting for transfers between devices, shards(): part = lax.all_gather(part, 'core', axis=0)  21.4 us
    all_gather x1, waiting for transfers between devices, shards(): first = lax.all_gather(along_z[:, :split], ('xhi', 'xlo'), axis=0)  19.6 us
    all_to_all x1, starting transfers between devices, shards(): lax.all_to_all(hidden.reshape(group_size, per_pixel, middle), FRAME_AXES,...  13.4 us
    dot_general x9, matrix products, shards(): lax.dot_general(patch, halves[row // split][:, row % split:row % split +...  10.5 us
    all_to_all x1, waiting for transfers between devices, shards(): lax.all_to_all(hidden.reshape(group_size, per_pixel, middle), FRAME_AXES,...  9.12 us
  transfers between devices with their start and end apart: 12, of which 8 were waited for; matrix products, arithmetic and copies ran while one was open for 32% of the time, Pallas kernels for 0%

profile of v6, /device:TPU:1, one launch (start us, length us, event | category | flops | bytes accessed | tf_op | source)
XLA Modules:
  0.0 294.6 jit_solution(13042043404901468989)
XLA Ops:
  18.5 8.8 %collective-permute-start.1 = (bf16[8,1,1024]{2,0,1:T(8,128)(2,1)S(1)}, bf16[8,1,1024]{2,0,1:T(8,128)(2,1)S(1)}, u32[]{:S(2)}, u32[]{:S(2)}) collective-permute-start(bf16[8,1,1024]{2,0,1:T(8,128)(2,1)S(1)} %copy.130), channel_id=1, source_target_pairs={{1,0},{2,1},{3,2},{5,4},{6,5},{7,6},{9,8},{10,9},{11,10},{13,12},{... | collective-permute-start | bytes 49160 | tf_op jit(solution)/shard_map/ppermute | solution.py:25
  33.7 5.0 %broadcast_multiply_fusion = (bf16[8,34,1024]{1,2,0:T(8,128)(2,1)S(1)}, bf16[8,34,1024]{1,2,0:T(8,128)(2,1)S(1)}) fusion(bf16[8]{0:T(256)(128)(2,1)S(1)} %and_convert_fusion.1, bf16[8,1,1024]{1,2,0:T(8,128)(2,1)} %copy.132, bf16[8,32,1024]{1,2,0:T(8,128)(2,1)} %bitcast.119, bf16[8,1,1024]{1,2,0:T(8,128)(2,1)} %copy.131), kind=kLoop, calls=%fused_computation.39 | loop fusion | flops 2506752 | bytes 1671184 | tf_op jit(solution)/shard_map/mul | solution.py:116
  44.2 7.7 %collective-permute-done.2 = bf16[1,34,1024]{1,2,0:T(8,128)(2,1)} collective-permute-done((bf16[1,34,1024]{1,2,0:T(8,128)(2,1)S(1)}, bf16[1,34,1024]{1,2,0:T(8,128)(2,1)}, u32[]{:S(2)}, u32[]{:S(2)}) %collective-permute-start.2) | collective-permute-done | bytes 69664 | tf_op jit(solution)/shard_map/ppermute | solution.py:35
  56.1 3.4 %copy.135 = bf16[8,32,1024]{1,0,2:T(8,128)(2,1)} copy(bf16[8,32,1024]{2,1,0:T(8,128)(2,1)} %get-tuple-element.27) | data formatting | bytes 1048576 | tf_op jit(solution)/shard_map/slice | solution.py:122
  59.5 3.8 %reshape.151 = bf16[256,128,8]{0,2,1:T(8,128)(2,1)} reshape(bf16[8,32,1024]{1,0,2:T(8,128)(2,1)} %copy.135) | data formatting | bytes 1048576 | tf_op jit(solution)/shard_map/reshape | solution.py:123
  63.3 3.4 %copy.136 = bf16[8,32,1024]{1,0,2:T(8,128)(2,1)} copy(bf16[8,32,1024]{2,1,0:T(8,128)(2,1)} %get-tuple-element.26) | data formatting | bytes 1048576 | tf_op jit(solution)/shard_map/slice | solution.py:122
  66.7 3.8 %reshape.152 = bf16[256,128,8]{0,2,1:T(8,128)(2,1)} reshape(bf16[8,32,1024]{1,0,2:T(8,128)(2,1)} %copy.136) | data formatting | bytes 1048576 | tf_op jit(solution)/shard_map/reshape | solution.py:123
  70.5 2.5 copy.137
  72.9 3.8 %reshape.153 = bf16[256,128,8]{0,2,1:T(8,128)(2,1)} reshape(bf16[8,32,1024]{1,0,2:T(8,128)(2,1)} %copy.137) | data formatting | bytes 1048576 | tf_op jit(solution)/shard_map/reshape | solution.py:123
  78.0 2.7 fusion.48
  80.7 4.3 %collective-permute-start.3 = (bf16[16,48,512]{2,1,0:T(8,128)(2,1)}, bf16[16,48,512]{2,1,0:T(8,128)(2,1)}, u32[]{:S(2)}, u32[]{:S(2)}) collective-permute-start(bf16[16,48,512]{2,1,0:T(8,128)(2,1)} %get-tuple-element.21), channel_id=1, source_target_pairs={{0,66},{2,0},{64,2},{66,64},{1,67},{3,1},{65,3},{67,65},{4,70},{6,... | collective-permute-start | bytes 2359304 | tf_op jit(solution)/shard_map/ppermute | solution.py:51
  86.9 7.3 %collective-permute-done.3 = bf16[16,48,512]{2,1,0:T(8,128)(2,1)} collective-permute-done((bf16[16,48,512]{2,1,0:T(8,128)(2,1)}, bf16[16,48,512]{2,1,0:T(8,128)(2,1)}, u32[]{:S(2)}, u32[]{:S(2)}) %collective-permute-start.3) | collective-permute-done | bytes 786464 | tf_op jit(solution)/shard_map/ppermute | solution.py:51
  95.3 5.0 %collective-permute-start.6 = (bf16[16,24,512]{2,1,0:T(8,128)(2,1)S(1)}, bf16[16,24,512]{2,1,0:T(8,128)(2,1)S(1)}, u32[]{:S(2)}, u32[]{:S(2)}) collective-permute-start(bf16[16,24,512]{2,1,0:T(8,128)(2,1)S(1)} %slice.136), channel_id=1, source_target_pairs={{0,66},{2,0},{64,2},{66,64},{1,67},{3,1},{65,3},{67,65},{4,70},{6,... | collective-permute-start | bytes 1179656 | tf_op jit(solution)/shard_map/ppermute | solution.py:54
  100.4 2.2 collective-permute-start.5
  105.1 7.2 %collective-permute-done.6 = bf16[16,24,512]{2,1,0:T(8,128)(2,1)S(1)} collective-permute-done((bf16[16,24,512]{2,1,0:T(8,128)(2,1)S(1)}, bf16[16,24,512]{2,1,0:T(8,128)(2,1)S(1)}, u32[]{:S(2)}, u32[]{:S(2)}) %collective-permute-start.6) | collective-permute-done | bytes 393248 | tf_op jit(solution)/shard_map/ppermute | solution.py:54
  112.3 9.0 %collective-permute-done.5 = bf16[16,24,512]{2,1,0:T(8,128)(2,1)S(1)} collective-permute-done((bf16[16,24,512]{2,1,0:T(8,128)(2,1)S(1)}, bf16[16,24,512]{2,1,0:T(8,128)(2,1)S(1)}, u32[]{:S(2)}, u32[]{:S(2)}) %collective-permute-start.5) | collective-permute-done | bytes 393248 | tf_op jit(solution)/shard_map/ppermute | solution.py:53
  124.8 19.6 %all-gather.11.cloned.1.call-done = bf16[64,48,512]{2,1,0:T(8,128)(2,1)} async-done(((bf16[16,48,512]{2,1,0:T(8,128)(2,1)}), bf16[64,48,512]{2,1,0:T(8,128)(2,1)}) %all-gather.11.cloned.1.call-update) | async-done | bytes 3145744 | tf_op jit(solution)/shard_map/all_gather | solution.py:128
  144.5 3.3 %fusion.46 = (bf16[8,32,1024]{1,2,0:T(8,128)(2,1)}, bf16[8,32,1024]{1,2,0:T(8,128)(2,1)S(1)}, bf16[8,32,1024]{1,2,0:T(8,128)(2,1)}) fusion(bf16[8,34,1024]{1,2,0:T(8,128)(2,1)S(1)} %get-tuple-element.13), kind=kLoop, calls=%fused_computation.84 | loop fusion | bytes 3145728 | tf_op jit(solution)/shard_map/slice | solution.py:122
  149.2 2.2 reshape.156
  151.3 2.9 copy.138
  154.3 2.2 reshape.155
  156.4 3.3 %copy.140 = bf16[8,32,1024]{1,0,2:T(8,128)(2,1)S(1)} copy(bf16[8,32,1024]{1,2,0:T(8,128)(2,1)} %get-tuple-element.15) | data formatting | bytes 1048576 | tf_op jit(solution)/shard_map/slice | solution.py:122
  163.1 2.6 copy.145
  165.7 2.2 reshape.161
  169.5 2.2 reshape.158
  178.7 21.4 %all-gather.13.cloned.1.call-done = bf16[8,16,48,512]{3,2,1,0:T(8,128)(2,1)} async-done(((bf16[4,16,48,512]{3,2,1,0:T(8,128)(2,1)}), bf16[8,16,48,512]{3,2,1,0:T(8,128)(2,1)}) %all-gather.13.cloned.1.call-update) | async-done | bytes 6291472 | tf_op jit(solution)/shard_map/all_gather | solution.py:132
  208.0 2.6 fusion.35
  210.6 13.4 %all-to-all-start = ((bf16[16,16,512]{2,1,0:T(8,128)(2,1)}), bf16[16,16,512]{2,1,0:T(8,128)(2,1)S(1)}, u32[]{:S(2)}, u32[]{:S(2)}) async-start(bf16[16,16,512]{2,1,0:T(8,128)(2,1)} %bitcast.22), calls=%async_computation | async-start | bytes 524288 | tf_op jit(solution)/shard_map/all_to_all | solution.py:146
  227.4 3.5 %copy.149 = bf16[2,16,2,2,8,3,512]{6,4,3,2,1,0,5:T(8,128)(2,1)} copy(bf16[2,16,2,2,8,3,512]{6,1,2,0,3,5,4:T(8,128)(2,1)S(1)} %bitcast.120) | data formatting | bytes 6291456 | tf_op jit(solution)/shard_map/transpose | solution.py:162
  230.9 9.1 %all-to-all-done = bf16[16,16,512]{2,1,0:T(8,128)(2,1)S(1)} async-done(((bf16[16,16,512]{2,1,0:T(8,128)(2,1)}), bf16[16,16,512]{2,1,0:T(8,128)(2,1)S(1)}, u32[]{:S(2)}, u32[]{:S(2)}) %all-to-all-start) | async-done | bytes 262176 | tf_op jit(solution)/shard_map/all_to_all | solution.py:146
  243.2 3.0 %fusion.1 = bf16[256,1024]{1,0:T(8,128)(2,1)S(1)} fusion(bf16[256,3,512]{2,0,1:T(8,128)(2,1)S(1)} %reshape.164, bf16[1024,3,512]{2,0,1:T(8,128)(2,1)} %bitcast.126), kind=kOutput, calls=%fused_computation.7 | convolution fusion | flops 805568512 | bytes 4456448 | tf_op jit(solution)/shard_map/dot_general | solution.py:163
  246.2 40.9 %all_to_all.10 = bf16[16,16,1024]{2,1,0:T(8,128)(2,1)S(1)} all-to-all(bf16[16,16,1024]{2,1,0:T(8,128)(2,1)S(1)} %bitcast.133), channel_id=1, replica_groups=mesh['clip'=4,'xhi'=2,'zhi'=8,'zlo'=2,'xlo'=2,'core'=2] {'xhi','zhi'}, dimensions={0} | all-to-all | bytes 1048576 | tf_op jit(solution)/shard_map/all_to_all | solution.py:167
  (105 shorter events, 66.9 us)
Async XLA Ops:
  6.5 71.4 %all-gather.9.cloned.1.call-start = ((), (), s32[]{:S(2)}) async-start(), calls=%async_computation.2 | async-start | bytes 1671168 | tf_op jit(solution)/shard_map/all_gather | solution.py:94
  8.9 135.6 %all-gather.11.cloned.1.call-start = ((), (), s32[]{:S(2)}) async-start(), calls=%async_computation.3 | async-start | bytes 3932160 | tf_op jit(solution)/shard_map/all_gather | solution.py:128
  14.4 2.1 copy-start
  18.5 11.7 %collective-permute-start.1 = (bf16[8,1,1024]{2,0,1:T(8,128)(2,1)S(1)}, bf16[8,1,1024]{2,0,1:T(8,128)(2,1)S(1)}, u32[]{:S(2)}, u32[]{:S(2)}) collective-permute-start(bf16[8,1,1024]{2,0,1:T(8,128)(2,1)S(1)} %copy.130), channel_id=1, source_target_pairs={{1,0},{2,1},{3,2},{5,4},{6,5},{7,6},{9,8},{10,9},{11,10},{13,12},{... | collective-permute-start | bytes 49160 | tf_op jit(solution)/shard_map/ppermute | solution.py:25
  28.2 3.8 %collective-permute-start = (bf16[8,1,1024]{2,0,1:T(8,128)(2,1)S(1)}, bf16[8,1,1024]{2,0,1:T(8,128)(2,1)S(1)}, u32[]{:S(2)}, u32[]{:S(2)}) collective-permute-start(bf16[8,1,1024]{2,0,1:T(8,128)(2,1)S(1)} %copy.129), channel_id=1, source_target_pairs={{0,1},{1,2},{2,3},{4,5},{5,6},{6,7},{8,9},{9,10},{10,11},{12,13},{... | collective-permute-start | bytes 49160 | tf_op jit(solution)/shard_map/ppermute | solution.py:23
  38.8 1.4 copy-start.1
  40.2 11.7 %collective-permute-start.2 = (bf16[1,34,1024]{1,2,0:T(8,128)(2,1)S(1)}, bf16[1,34,1024]{1,2,0:T(8,128)(2,1)}, u32[]{:S(2)}, u32[]{:S(2)}) collective-permute-start(bf16[1,34,1024]{1,2,0:T(8,128)(2,1)S(1)} %slice_select_fusion), channel_id=1, source_target_pairs={{0,4},{4,0},{8,12},{12,8},{16,20},{20,16},{24,28},{28,24},{32,36},... | collective-permute-start | bytes 208904 | tf_op jit(solution)/shard_map/ppermute | solution.py:35
  80.7 94.3 %all-gather.15.cloned.1.call-start = ((), (), s32[]{:S(2)}) async-start(), calls=%async_computation.5 | async-start | bytes 9437184 | tf_op jit(solution)/shard_map/all_gather | solution.py:132
  80.7 13.5 %collective-permute-start.3 = (bf16[16,48,512]{2,1,0:T(8,128)(2,1)}, bf16[16,48,512]{2,1,0:T(8,128)(2,1)}, u32[]{:S(2)}, u32[]{:S(2)}) collective-permute-start(bf16[16,48,512]{2,1,0:T(8,128)(2,1)} %get-tuple-element.21), channel_id=1, source_target_pairs={{0,66},{2,0},{64,2},{66,64},{1,67},{3,1},{65,3},{67,65},{4,70},{6,... | collective-permute-start | bytes 2359304 | tf_op jit(solution)/shard_map/ppermute | solution.py:51
  85.0 15.3 %collective-permute-start.4 = (bf16[16,48,512]{2,1,0:T(8,128)(2,1)}, bf16[16,48,512]{2,1,0:T(8,128)(2,1)S(1)}, u32[]{:S(2)}, u32[]{:S(2)}) collective-permute-start(bf16[16,48,512]{2,1,0:T(8,128)(2,1)} %get-tuple-element.21), channel_id=1, source_target_pairs={{0,2},{2,64},{64,66},{66,0},{1,3},{3,65},{65,67},{67,1},{4,6},{6,6... | collective-permute-start | bytes 2359304 | tf_op jit(solution)/shard_map/ppermute | solution.py:50
  95.3 17.0 %collective-permute-start.6 = (bf16[16,24,512]{2,1,0:T(8,128)(2,1)S(1)}, bf16[16,24,512]{2,1,0:T(8,128)(2,1)S(1)}, u32[]{:S(2)}, u32[]{:S(2)}) collective-permute-start(bf16[16,24,512]{2,1,0:T(8,128)(2,1)S(1)} %slice.136), channel_id=1, source_target_pairs={{0,66},{2,0},{64,2},{66,64},{1,67},{3,1},{65,3},{67,65},{4,70},{6,... | collective-permute-start | bytes 1179656 | tf_op jit(solution)/shard_map/ppermute | solution.py:54
  100.3 21.1 %copy-start.3 = (bf16[1536,512]{1,0:T(8,128)(2,1)S(1)}, bf16[1536,512]{1,0:T(8,128)(2,1)}, u32[]{:S(2)}) copy-start(bf16[1536,512]{1,0:T(8,128)(2,1)} %all-gather.9.cloned.1.call-done) | copy-start | bytes 4718596
  100.4 20.9 %collective-permute-start.5 = (bf16[16,24,512]{2,1,0:T(8,128)(2,1)S(1)}, bf16[16,24,512]{2,1,0:T(8,128)(2,1)S(1)}, u32[]{:S(2)}, u32[]{:S(2)}) collective-permute-start(bf16[16,24,512]{2,1,0:T(8,128)(2,1)S(1)} %slice.135), channel_id=1, source_target_pairs={{0,2},{2,64},{64,66},{66,0},{1,3},{3,65},{65,67},{67,1},{4,6},{6,6... | collective-permute-start | bytes 1179656 | tf_op jit(solution)/shard_map/ppermute | solution.py:53
  124.8 75.3 %all-gather.13.cloned.1.call-start = ((), (), s32[]{:S(2)}) async-start(), calls=%async_computation.4 | async-start | bytes 9437184 | tf_op jit(solution)/shard_map/all_gather | solution.py:132
  163.1 4.8 %copy-start.4 = (bf16[8,32,1024]{2,1,0:T(8,128)(2,1)S(1)}, bf16[8,32,1024]{2,1,0:T(8,128)(2,1)}, u32[]{:S(2)}) copy-start(bf16[8,32,1024]{2,1,0:T(8,128)(2,1)} %get-tuple-element.24) | copy-start | bytes 1572868
  175.0 1.9 copy-start.11
  176.9 23.1 %copy-start.10 = (bf16[256,128,8]{0,2,1:T(8,128)(2,1)S(1)}, bf16[256,128,8]{0,2,1:T(8,128)(2,1)}, u32[]{:S(2)}) copy-start(bf16[256,128,8]{0,2,1:T(8,128)(2,1)} %reshape.156) | copy-start | bytes 1572868
  200.1 1.9 copy-start.7
  200.1 3.3 %copy-start.14 = (bf16[8,16,48,512]{3,2,1,0:T(8,128)(2,1)S(1)}, bf16[8,16,48,512]{3,2,1,0:T(8,128)(2,1)}, u32[]{:S(2)}) copy-start(bf16[8,16,48,512]{3,2,1,0:T(8,128)(2,1)} %all-gather.13.cloned.1.call-done) | copy-start | bytes 18874372
  203.4 1.0 copy-start.6
  204.4 1.0 copy-start.5
  205.4 1.0 copy-start.8
  206.5 1.0 copy-start.9
  208.0 16.0 %copy-start.13 = (s32[8]{0:T(128)S(1)}, s32[8]{0:T(128)}, u32[]{:S(2)}) copy-start(s32[8]{0:T(128)} %param.9) | copy-start | bytes 100
  208.0 16.1 %copy-start.12 = (s32[16]{0:T(128)S(1)}, s32[16]{0:T(128)}, u32[]{:S(2)}) copy-start(s32[16]{0:T(128)} %param.8) | copy-start | bytes 196
  210.6 29.4 %all-to-all-start = ((bf16[16,16,512]{2,1,0:T(8,128)(2,1)}), bf16[16,16,512]{2,1,0:T(8,128)(2,1)S(1)}, u32[]{:S(2)}, u32[]{:S(2)}) async-start(bf16[16,16,512]{2,1,0:T(8,128)(2,1)} %bitcast.22), calls=%async_computation | async-start | bytes 524288 | tf_op jit(solution)/shard_map/all_to_all | solution.py:146
  243.2 43.9 %copy-start.2 = (bf16[8,32,1024]{2,1,0:T(8,128)(2,1)S(1)}, bf16[8,32,1024]{2,1,0:T(8,128)(2,1)}, u32[]{:S(2)}) copy-start(bf16[8,32,1024]{2,1,0:T(8,128)(2,1)} %param.5) | copy-start | bytes 1572868
Sparse Core Ops, SparseCore 0:
  9.4 68.4 all-gather.8
  80.8 63.6 all-gather.10
  146.5 22.9 all-gather.14
  171.5 28.5 all-gather.12
